TPU v7x, 256 devices: a whole 4x4x8 slice. The times are simulated.
256 devices in a mesh: dp: 32 (over x, z), own: 8 (over y, core).
Axes of the slice: x: 4, y: 4, z: 8, core: 2. Of those that a mesh axis runs over, the one named last changes fastest.
Arguments:
- partials: bfloat16 [32, 64, 256, 1024], P('dp', None, None, 'own')
- owner: int32 [64, 1], replicated, may hold values from 0 to 31; in each aligned block of 64 rows (0 to 63, 64 to 127, ...) at most 4 rows name the same one
- momentum: float32 [32, 4, 256, 1024], P('dp', None, None, 'own'), may hold values from -1.2 to 1.2
- master: float32 [32, 4, 256, 1024], P('dp', None, None, 'own'), may hold values from -0.3 to 0.3
Outputs:
- new_momentum: float32 [32, 4, 256, 1024], P('dp', None, None, 'own')
- new_master: float32 [32, 4, 256, 1024], P('dp', None, None, 'own')
- new_weights: bfloat16 [64, 256, 1024], P(None, None, 'own')
Inputs may be any that keep to these rules, and one draw needn't show every extreme that they name: `owner`: every group owns at least one block and at most 4 blocks; some group owns exactly 4.
All inputs are finite; a program needn't handle non-finite values.
Results may differ from a plain program's by a relative error of at most 0.0007.
Values may be sent and summed in bfloat16 or wider, within the bound.
No kernel may reach another device: no remote copies, remote signals or barrier semaphores. Data moves between devices by JAX's collectives and lax.ppermute only.
A program may use at most 128 MiB of HBM per device.

v0:
```python
import math

import jax
import jax.numpy as jnp
from jax import lax
from jax.sharding import PartitionSpec as P

D = 1024
ITERS = 5


COEF_A = 3.4445
COEF_B = -4.775
COEF_C = 2.0315
BETA = 0.95
STEP_SIZE = 0.2
DECAY = 0.1
EPSILON = 1e-07


def slot_targets(owner_list, group_count, slot_count):
    onehot = (owner_list[:, None] == jnp.arange(group_count, dtype=jnp.int32)[None, :]).astype(
        jnp.int32
    )
    before = jnp.cumsum(onehot, axis=0) - onehot
    ranks = jnp.sum(before * onehot, axis=1)
    return owner_list * slot_count + ranks


def slot_sources(target, slot_count, block_count):
    positions = jnp.arange(slot_count, dtype=jnp.int32)
    matches = positions[:, None] == target[None, :]
    present = jnp.any(matches, axis=1)
    source = jnp.sum(
        jnp.where(matches, jnp.arange(block_count, dtype=jnp.int32)[None, :], 0), axis=1
    )
    return (present, source)


def local_gram(values):
    return jnp.einsum(
        "srk,stk->srt",
        values,
        values,
        precision=lax.Precision.HIGHEST,
        preferred_element_type=jnp.float32,
    )


def gram_total(values):
    return lax.psum(local_gram(values), "own")


def newton_turn(ortho, gram):
    square = jnp.einsum(
        "srt,stu->sru",
        gram,
        gram,
        precision=lax.Precision.HIGHEST,
        preferred_element_type=jnp.float32,
    )
    poly = COEF_B * gram + COEF_C * square
    product = jnp.einsum(
        "srt,stk->srk",
        poly,
        ortho,
        precision=lax.Precision.HIGHEST,
        preferred_element_type=jnp.float32,
    )
    return COEF_A * ortho + product


def on_device(partials, owner, momentum, master):
    group_count = lax.axis_size("dp")
    local_rows = partials[0]
    block_count = local_rows.shape[0]
    slot_count = momentum.shape[1]
    block_rows = momentum.shape[2]
    owner_list = owner[:, 0]
    target = slot_targets(owner_list, group_count, slot_count)
    present, source = slot_sources(target, group_count * slot_count, block_count)
    outgoing = jnp.where(
        present[:, None, None], jnp.take(local_rows, source, axis=0).astype(jnp.float32), 0.0
    )
    gradient = lax.psum_scatter(outgoing, "dp", scatter_dimension=0, tiled=True)
    momentum_new = BETA * momentum[0] + gradient
    update = gradient + BETA * momentum_new
    squares = lax.psum(jnp.sum(update * update, axis=(1, 2)), "own")
    factor = 1.0 / (jnp.sqrt(squares) + EPSILON)
    ortho = update * factor[:, None, None]
    gram = gram_total(ortho)
    for iteration in range(ITERS):
        if iteration > 0:
            gram = gram_total(ortho)
        ortho = newton_turn(ortho, gram)
    step_factor = STEP_SIZE * 0.2 * math.sqrt(max(block_rows, D))
    master_new = master[0] * (1.0 - STEP_SIZE * DECAY) - step_factor * ortho
    weights_low = master_new.astype(jnp.bfloat16)
    every_slot = lax.all_gather(weights_low, "dp", axis=0, tiled=True)
    weights = jnp.take(every_slot, target, axis=0)
    return (momentum_new[None], master_new[None], weights)


def solution(mesh):
    in_specs = (
        P("dp", None, None, "own"),
        P(),
        P("dp", None, None, "own"),
        P("dp", None, None, "own"),
    )
    out_specs = (P("dp", None, None, "own"), P("dp", None, None, "own"), P(None, None, "own"))
    return jax.shard_map(
        on_device, mesh=mesh, in_specs=in_specs, out_specs=out_specs, check_vma=False
    )
```

profile of v0, /device:TPU:1, one launch (start us, length us, event | category | flops | bytes accessed | tf_op | source)
XLA Modules:
  0.0 780.1 jit_solution(16891098648073873890)
XLA Ops:
  9.8 8.6 %gather_fusion = bf16[128,256,128]{2,1,0:T(8,128)(2,1)} fusion(bf16[64,256,128]{2,1,0:T(8,128)(2,1)} %bitcast.64, s32[1024]{0:T(1024)S(1)} %pad_clamp_fusion.1), kind=kCustom, calls=%fused_computation | custom fusion | bytes 16777728 | tf_op jit(solution)/shard_map/jit(_take)/gather | solution.py:83
  18.4 13.4 %convert_select_fusion = f32[128,256,128]{2,1,0:T(8,128)} fusion(bf16[128,256,128]{2,1,0:T(8,128)(2,1)} %gather_fusion, pred[128]{0:T(512)(128)(4,1)S(1)} %compare_and_fusion, pred[128]{0:T(512)(128)(4,1)S(1)} %fusion.14), kind=kLoop, calls=%fused_computation.2 | loop fusion | flops 12582912 | bytes 25166080 | tf_op jit(solution)/shard_map/jit(_where)/select_n | solution.py:82
  31.8 245.8 %reduce-scatter.2.cloned.1.call-done = f32[4,256,128]{2,1,0:T(8,128)} async-done(((f32[128,256,128]{2,1,0:T(8,128)}), f32[4,256,128]{2,1,0:T(8,128)}) %reduce-scatter.2.cloned.1.call-update) | async-done | bytes 524304 | tf_op jit(solution)/shard_map/reduce_scatter | solution.py:85
  279.6 17.0 %psum.42 = f32[4]{0:T(128)S(1)} all-reduce(f32[4]{0:T(128)S(1)} %get-tuple-element.5), channel_id=1, replica_groups=mesh['dp'=32,'own'=8] {'own'}, use_global_device_ids=true, to_apply=%region_6.7 | all-reduce | flops 4 | bytes 32 | tf_op jit(solution)/shard_map/psum | solution.py:88
  296.6 3.3 fusion.7
  300.0 61.9 %all-reduce.6.cloned.1.call-done = f32[4,256,256]{2,1,0:T(8,128)} async-done(((f32[4,256,256]{2,1,0:T(8,128)}), f32[4,256,256]{2,1,0:T(8,128)}) %all-reduce.6.cloned.1.call-update) | async-done | bytes 1048592 | tf_op jit(solution)/shard_map/psum | solution.py:51
  361.9 3.3 fusion.4
  365.2 2.4 convolution_add_fusion.4
  367.6 2.0 fusion.17
  369.8 67.1 %all-reduce.8.cloned.1.call-done = f32[4,256,256]{2,1,0:T(8,128)} async-done(((f32[4,256,256]{2,1,0:T(8,128)}), f32[4,256,256]{2,1,0:T(8,128)}) %all-reduce.8.cloned.1.call-update) | async-done | bytes 1048592 | tf_op jit(solution)/shard_map/psum | solution.py:51
  437.0 3.3 fusion.3
  441.3 2.0 fusion.18
  443.4 67.3 %all-reduce.10.cloned.1.call-done = f32[4,256,256]{2,1,0:T(8,128)} async-done(((f32[4,256,256]{2,1,0:T(8,128)}), f32[4,256,256]{2,1,0:T(8,128)}) %all-reduce.10.cloned.1.call-update) | async-done | bytes 1048592 | tf_op jit(solution)/shard_map/psum | solution.py:51
  510.7 3.3 fusion.2
  515.1 2.0 fusion.19
  517.1 67.3 %all-reduce.12.cloned.1.call-done = f32[4,256,256]{2,1,0:T(8,128)} async-done(((f32[4,256,256]{2,1,0:T(8,128)}), f32[4,256,256]{2,1,0:T(8,128)}) %all-reduce.12.cloned.1.call-update) | async-done | bytes 1048592 | tf_op jit(solution)/shard_map/psum | solution.py:51
  584.5 3.3 fusion.1
  588.8 2.0 fusion.20
  591.1 67.1 %all-reduce.14.cloned.1.call-done = f32[4,256,256]{2,1,0:T(8,128)} async-done(((f32[4,256,256]{2,1,0:T(8,128)}), f32[4,256,256]{2,1,0:T(8,128)}) %all-reduce.14.cloned.1.call-update) | async-done | bytes 1048592 | tf_op jit(solution)/shard_map/psum | solution.py:51
  658.2 3.3 fusion
  661.5 2.0 fusion.16
  663.6 98.5 %all-gather.2.cloned.1.call-done = bf16[128,256,128]{2,1,0:T(8,128)(2,1)} async-done(((bf16[4,256,128]{2,1,0:T(8,128)(2,1)}), bf16[128,256,128]{2,1,0:T(8,128)(2,1)}) %all-gather.2.cloned.1.call-update) | async-done | bytes 8388624 | tf_op jit(solution)/shard_map/all_gather | solution.py:99
  762.1 6.5 gather_fusion.1
  768.6 4.6 broadcast_select_fusion
  (36 shorter events, 8.5 us)
Async XLA Ops:
  7.2 270.5 %reduce-scatter.2.cloned.1.call-start = ((), (), s32[]{:S(2)}) async-start(), calls=%async_computation.1 | async-start | bytes 17301504 | tf_op jit(solution)/shard_map/reduce_scatter | solution.py:85
  31.8 245.9 %copy-start = (f32[1,4,256,128]{3,2,1,0:T(8,128)S(1)}, f32[1,4,256,128]{3,2,1,0:T(8,128)}, u32[]{:S(2)}) copy-start(f32[1,4,256,128]{3,2,1,0:T(8,128)} %param.6) | copy-start | bytes 1572868
  31.8 330.1 %all-reduce.6.cloned.1.call-start = ((), (), s32[]{:S(2)}) async-start(), calls=%async_computation.2 | async-start | bytes 2097152 | tf_op jit(solution)/shard_map/psum | solution.py:51
  300.0 137.0 %all-reduce.8.cloned.1.call-start = ((), (), s32[]{:S(2)}) async-start(), calls=%async_computation.3 | async-start | bytes 2097152 | tf_op jit(solution)/shard_map/psum | solution.py:51
  369.6 141.1 %all-reduce.10.cloned.1.call-start = ((), (), s32[]{:S(2)}) async-start(), calls=%async_computation.4 | async-start | bytes 2097152 | tf_op jit(solution)/shard_map/psum | solution.py:51
  443.3 141.2 %all-reduce.12.cloned.1.call-start = ((), (), s32[]{:S(2)}) async-start(), calls=%async_computation.5 | async-start | bytes 2097152 | tf_op jit(solution)/shard_map/psum | solution.py:51
  514.0 147.5 %copy-start.1 = (f32[1,4,256,128]{3,2,1,0:T(8,128)S(1)}, f32[1,4,256,128]{3,2,1,0:T(8,128)}, u32[]{:S(2)}) copy-start(f32[1,4,256,128]{3,2,1,0:T(8,128)} %param.7) | copy-start | bytes 1572868
  517.1 146.5 %copy-start.2 = (s32[64,1]{0,1:T(1,128)S(1)}, s32[64,1]{0,1:T(1,128)}, u32[]{:S(2)}) copy-start(s32[64,1]{0,1:T(1,128)} %param.5) | copy-start | bytes 772
  517.1 141.1 %all-reduce.14.cloned.1.call-start = ((), (), s32[]{:S(2)}) async-start(), calls=%async_computation.6 | async-start | bytes 2097152 | tf_op jit(solution)/shard_map/psum | solution.py:51
  590.8 171.3 %all-gather.2.cloned.1.call-start = ((), (), s32[]{:S(2)}) async-start(), calls=%async_computation.7 | async-start | bytes 8650752 | tf_op jit(solution)/shard_map/all_gather | solution.py:99
Sparse Core Ops, SparseCore 0:
  31.9 245.7 reduce-scatter.1
  300.1 61.7 all-reduce.5
  369.7 67.2 all-reduce.7
  443.4 67.2 all-reduce.9
  517.2 67.2 all-reduce.11
  591.0 67.2 all-reduce.13
  663.7 98.4 all-gather.1
where the time goes:
time: 781 us; the launch traced here: 780 us
  waiting for transfers between devices  675 us (86%)
  matrix products  35.2 us (5%)
  other arithmetic  22.5 us (3%)
  blocking collectives  17 us (2%)
  local copies, waits for them, and re-layouts  15.1 us (2%)
  between operations  14.3 us (2%)
    psum x5, waiting for transfers between devices, gram_total(): return lax.psum(local_gram(values), 'own')  331 us
    reduce_scatter x1, waiting for transfers between devices, on_device(): gradient = lax.psum_scatter(outgoing, 'dp', scatter_dimension=0, tiled=True)  246 us
    all_gather x1, waiting for transfers between devices, on_device(): every_slot = lax.all_gather(weights_low, 'dp', axis=0, tiled=True)  98.5 us
    psum x1, blocking collectives, on_device(): squares = lax.psum(jnp.sum(update * update, axis=(1, 2)), 'own')  17 us
    dot_general x5, matrix products, newton_turn(): jnp.einsum('srt,stu->sru', gram, gram, precision=lax.Precision.HIGHEST, p...  16.5 us
  transfers between devices with their start and end apart: 7, of which 7 were waited for; matrix products, arithmetic and copies ran while one was open for 0% of the time, Pallas kernels for 0%

commit v1 on v0

--- a/solution.py
+++ b/solution.py
@@ -51,14 +51,18 @@
     return lax.psum(local_gram(values), "own")
 
 
-def newton_turn(ortho, gram):
-    square = jnp.einsum(
+def matmul(left, right):
+    return jnp.einsum(
         "srt,stu->sru",
-        gram,
-        gram,
+        left,
+        right,
         precision=lax.Precision.HIGHEST,
         preferred_element_type=jnp.float32,
     )
+
+
+def newton_turn(ortho, gram, eye, next_gram):
+    square = matmul(gram, gram)
     poly = COEF_B * gram + COEF_C * square
     product = jnp.einsum(
         "srt,stk->srk",
@@ -67,7 +71,11 @@
         precision=lax.Precision.HIGHEST,
         preferred_element_type=jnp.float32,
     )
-    return COEF_A * ortho + product
+    ortho = COEF_A * ortho + product
+    if next_gram:
+        step = COEF_A * eye + poly
+        gram = matmul(step, matmul(gram, step))
+    return ortho, gram
 
 
 def on_device(partials, owner, momentum, master):
@@ -85,14 +93,14 @@
     gradient = lax.psum_scatter(outgoing, "dp", scatter_dimension=0, tiled=True)
     momentum_new = BETA * momentum[0] + gradient
     update = gradient + BETA * momentum_new
-    squares = lax.psum(jnp.sum(update * update, axis=(1, 2)), "own")
+    update_gram = gram_total(update)
+    squares = jnp.trace(update_gram, axis1=1, axis2=2)
     factor = 1.0 / (jnp.sqrt(squares) + EPSILON)
     ortho = update * factor[:, None, None]
-    gram = gram_total(ortho)
+    gram = update_gram * (factor * factor)[:, None, None]
+    eye = jnp.eye(block_rows, dtype=jnp.float32)[None]
     for iteration in range(ITERS):
-        if iteration > 0:
-            gram = gram_total(ortho)
-        ortho = newton_turn(ortho, gram)
+        ortho, gram = newton_turn(ortho, gram, eye, iteration < ITERS - 1)
     step_factor = STEP_SIZE * 0.2 * math.sqrt(max(block_rows, D))
     master_new = master[0] * (1.0 - STEP_SIZE * DECAY) - step_factor * ortho
     weights_low = master_new.astype(jnp.bfloat16)

time: 781 us -> 494 us (0.63)
  waiting for transfers between devices: 675 us -> 412 us
  blocking collectives: 17 us -> 0 us
    psum x5 -> x1, waiting for transfers between devices: 331 us -> 68.5 us  [gram_total(): return lax.psum(local_gram(values), 'own')]
    psum x1 -> x0, blocking collectives: 17 us -> none  [on_device(): squares = lax.psum(jnp.sum(update * update, axis=(1, 2)), 'own')]
    dot_general x5 -> x1, matrix products: 11.2 us -> 3.27 us  [local_gram(): jnp.einsum('srk,stk->srt', values, values, precision=lax.Precision.HIGHES...]
    dot_general x5 -> x13, matrix products: 16.5 us -> 19.5 us  [matmul(): jnp.einsum('srt,stu->sru', left, right, precision=lax.Precision.HIGHEST,...]
  transfers between devices with their start and end apart: 7 -> 3, of which waited for: 7 -> 3; matrix products, arithmetic and copies ran while one was open for 0% -> 0% of each run, Pallas kernels for 0% -> 0%
where the time goes in v1:
time: 494 us
  waiting for transfers between devices  412 us (83%)
  matrix products  29.2 us (6%)
  other arithmetic  22.9 us (5%)
  local copies, waits for them, and re-layouts  15.1 us (3%)
  between operations  14 us (3%)
    reduce_scatter x1, waiting for transfers between devices, on_device(): gradient = lax.psum_scatter(outgoing, 'dp', scatter_dimension=0, tiled=True)  246 us
    all_gather x1, waiting for transfers between devices, on_device(): every_slot = lax.all_gather(weights_low, 'dp', axis=0, tiled=True)  97.7 us
    psum x1, waiting for transfers between devices, gram_total(): return lax.psum(local_gram(values), 'own')  68.5 us
    dot_general x13, matrix products, matmul(): jnp.einsum('srt,stu->sru', left, right, precision=lax.Precision.HIGHEST,...  19.5 us
    select_n x1, other arithmetic, on_device(): jnp.where(present[:, None, None], jnp.take(local_rows, source, axis=0).as...  13.4 us
  transfers between devices with their start and end apart: 3, of which 3 were waited for; matrix products, arithmetic and copies ran while one was open for 0% of the time, Pallas kernels for 0%

profile of v1, /device:TPU:1, one launch (start us, length us, event | category | flops | bytes accessed | tf_op | source)
XLA Modules:
  0.0 493.5 jit_solution(1865720809806670317)
XLA Ops:
  9.8 8.6 %gather_fusion = bf16[128,256,128]{2,1,0:T(8,128)(2,1)} fusion(bf16[64,256,128]{2,1,0:T(8,128)(2,1)} %bitcast.57, s32[1024]{0:T(1024)S(1)} %pad_clamp_fusion.1), kind=kCustom, calls=%fused_computation | custom fusion | bytes 16777728 | tf_op jit(solution)/shard_map/jit(_take)/gather | solution.py:91
  18.4 13.4 %convert_select_fusion = f32[128,256,128]{2,1,0:T(8,128)} fusion(bf16[128,256,128]{2,1,0:T(8,128)(2,1)} %gather_fusion, pred[128]{0:T(512)(128)(4,1)S(1)} %compare_and_fusion, pred[128]{0:T(512)(128)(4,1)S(1)} %fusion.40), kind=kLoop, calls=%fused_computation.2 | loop fusion | flops 12582912 | bytes 25166080 | tf_op jit(solution)/shard_map/jit(_where)/select_n | solution.py:90
  31.8 245.8 %reduce-scatter.2.cloned.1.call-done = f32[4,256,128]{2,1,0:T(8,128)} async-done(((f32[128,256,128]{2,1,0:T(8,128)}), f32[4,256,128]{2,1,0:T(8,128)}) %reduce-scatter.2.cloned.1.call-update) | async-done | bytes 524304 | tf_op jit(solution)/shard_map/reduce_scatter | solution.py:93
  277.7 3.3 fusion.38
  281.3 68.5 %all-reduce.2.cloned.1.call-done = f32[4,256,256]{2,1,0:T(8,128)} async-done(((f32[4,256,256]{2,1,0:T(8,128)}), f32[4,256,256]{2,1,0:T(8,128)}) %all-reduce.2.cloned.1.call-update) | async-done | bytes 1048592 | tf_op jit(solution)/shard_map/psum | solution.py:51
  349.7 1.4 select_reduce_fusion
  351.2 3.4 fusion.4
  354.6 2.5 fusion.21
  357.1 1.2 fusion.19
  358.3 1.3 fusion.3
  359.6 1.2 fusion.17
  360.8 1.2 convolution_add_fusion.4
  363.0 1.2 fusion.15
  364.2 1.3 fusion.2
  365.5 1.4 fusion.13
  368.0 1.2 fusion.11
  369.2 1.3 fusion.1
  370.5 1.2 fusion.9
  372.8 1.2 fusion.7
  374.0 1.3 fusion
  375.3 2.0 fusion.45
  378.2 97.7 %all-gather.2.cloned.1.call-done = bf16[128,256,128]{2,1,0:T(8,128)(2,1)} async-done(((bf16[4,256,128]{2,1,0:T(8,128)(2,1)}), bf16[128,256,128]{2,1,0:T(8,128)(2,1)}) %all-gather.2.cloned.1.call-update) | async-done | bytes 8388624 | tf_op jit(solution)/shard_map/all_gather | solution.py:107
  475.9 6.5 %gather_fusion.1 = bf16[64,256,128]{2,1,0:T(8,128)(2,1)} fusion(bf16[128,256,128]{2,1,0:T(8,128)(2,1)} %all-gather.2.cloned.1.call-done, s32[1024]{0:T(1024)S(1)} %pad_clamp_fusion), kind=kCustom, calls=%fused_computation.1 | custom fusion | bytes 8388864 | tf_op jit(solution)/shard_map/jit(_take)/gather | solution.py:108
  482.4 4.6 broadcast_select_fusion
  (32 shorter events, 7.0 us)
Async XLA Ops:
  7.2 270.5 %reduce-scatter.2.cloned.1.call-start = ((), (), s32[]{:S(2)}) async-start(), calls=%async_computation.1 | async-start | bytes 17301504 | tf_op jit(solution)/shard_map/reduce_scatter | solution.py:93
  31.8 245.9 %copy-start = (f32[1,4,256,128]{3,2,1,0:T(8,128)S(1)}, f32[1,4,256,128]{3,2,1,0:T(8,128)}, u32[]{:S(2)}) copy-start(f32[1,4,256,128]{3,2,1,0:T(8,128)} %param.6) | copy-start | bytes 1572868
  31.8 318.0 %all-reduce.2.cloned.1.call-start = ((), (), s32[]{:S(2)}) async-start(), calls=%async_computation.2 | async-start | bytes 2097152 | tf_op jit(solution)/shard_map/psum | solution.py:51
  281.0 194.9 %all-gather.2.cloned.1.call-start = ((), (), s32[]{:S(2)}) async-start(), calls=%async_computation.3 | async-start | bytes 8650752 | tf_op jit(solution)/shard_map/all_gather | solution.py:107
  281.2 79.5 %copy-start.1 = (f32[4,256,128]{2,1,0:T(8,128)S(1)}, f32[4,256,128]{2,1,0:T(8,128)}, u32[]{:S(2)}) copy-start(f32[4,256,128]{2,1,0:T(8,128)} %reduce-scatter.2.cloned.1.call-done) | copy-start | bytes 1572868
  369.2 6.1 %copy-start.2 = (f32[1,4,256,128]{3,2,1,0:T(8,128)S(1)}, f32[1,4,256,128]{3,2,1,0:T(8,128)}, u32[]{:S(2)}) copy-start(f32[1,4,256,128]{3,2,1,0:T(8,128)} %param.7) | copy-start | bytes 1572868
  370.5 6.8 %copy-start.3 = (s32[64,1]{0,1:T(1,128)S(1)}, s32[64,1]{0,1:T(1,128)}, u32[]{:S(2)}) copy-start(s32[64,1]{0,1:T(1,128)} %param.5) | copy-start | bytes 772
Sparse Core Ops, SparseCore 0:
  31.9 245.7 reduce-scatter.1
  281.1 68.5 all-reduce.1
  377.4 98.4 all-gather.1

commit v2 on v1

--- a/solution.py
+++ b/solution.py
@@ -3,7 +3,7 @@
 import jax
 import jax.numpy as jnp
 from jax import lax
-from jax.sharding import PartitionSpec as P
+from jax.sharding import Mesh, PartitionSpec as P
 
 D = 1024
 ITERS = 5
@@ -79,7 +79,7 @@
 
 
 def on_device(partials, owner, momentum, master):
-    group_count = lax.axis_size("dp")
+    group_count = lax.axis_size("x") * lax.axis_size("z")
     local_rows = partials[0]
     block_count = local_rows.shape[0]
     slot_count = momentum.shape[1]
@@ -87,10 +87,12 @@
     owner_list = owner[:, 0]
     target = slot_targets(owner_list, group_count, slot_count)
     present, source = slot_sources(target, group_count * slot_count, block_count)
-    outgoing = jnp.where(
-        present[:, None, None], jnp.take(local_rows, source, axis=0).astype(jnp.float32), 0.0
-    )
-    gradient = lax.psum_scatter(outgoing, "dp", scatter_dimension=0, tiled=True)
+    outgoing = jnp.where(present[:, None, None], jnp.take(local_rows, source, axis=0), 0)
+    row_count = lax.axis_size("x")
+    outgoing = outgoing.reshape((row_count, -1) + outgoing.shape[1:])
+    arrived = lax.all_to_all(outgoing, "x", 0, 0, tiled=True)
+    row_sum = jnp.sum(arrived.astype(jnp.float32), axis=0)
+    gradient = lax.psum_scatter(row_sum, "z", scatter_dimension=0, tiled=True)
     momentum_new = BETA * momentum[0] + gradient
     update = gradient + BETA * momentum_new
     update_gram = gram_total(update)
@@ -104,19 +106,28 @@
     step_factor = STEP_SIZE * 0.2 * math.sqrt(max(block_rows, D))
     master_new = master[0] * (1.0 - STEP_SIZE * DECAY) - step_factor * ortho
     weights_low = master_new.astype(jnp.bfloat16)
-    every_slot = lax.all_gather(weights_low, "dp", axis=0, tiled=True)
+    every_slot = lax.all_gather(weights_low, ("x", "z"), axis=0, tiled=True)
     weights = jnp.take(every_slot, target, axis=0)
     return (momentum_new[None], master_new[None], weights)
 
 
+def split_mesh(mesh):
+    devices = mesh.devices
+    row_count = len({device.coords[0] for device in devices[:, 0]})
+    shape = (row_count, devices.shape[0] // row_count, devices.shape[1])
+    return Mesh(devices.reshape(shape), ("x", "z", "own"))
+
+
 def solution(mesh):
+    grid = split_mesh(mesh)
+    data = ("x", "z")
     in_specs = (
-        P("dp", None, None, "own"),
+        P(data, None, None, "own"),
         P(),
-        P("dp", None, None, "own"),
-        P("dp", None, None, "own"),
+        P(data, None, None, "own"),
+        P(data, None, None, "own"),
     )
-    out_specs = (P("dp", None, None, "own"), P("dp", None, None, "own"), P(None, None, "own"))
+    out_specs = (P(data, None, None, "own"), P(data, None, None, "own"), P(None, None, "own"))
     return jax.shard_map(
-        on_device, mesh=mesh, in_specs=in_specs, out_specs=out_specs, check_vma=False
+        on_device, mesh=grid, in_specs=in_specs, out_specs=out_specs, check_vma=False
     )

time: 494 us -> 394 us (0.80)
  waiting for transfers between devices: 412 us -> 220 us
  blocking collectives: 0 us -> 96.9 us
  other arithmetic: 22.9 us -> 17.8 us
    reduce_scatter x1, waiting for transfers between devices: 246 us -> 58.3 us  [on_device(): gradient = lax.psum_scatter(row_sum, 'z', scatter_dimension=0, tiled=True)]
    all_to_all x0 -> x1, blocking collectives: none -> 96.9 us  [on_device(): arrived = lax.all_to_all(outgoing, 'x', 0, 0, tiled=True)]
    select_n x2, other arithmetic: 13.4 us -> 4.67 us  [the longest x1 4.66 us: on_device(): jnp.where(present[:, None, None], jnp.take(local_rows, source, axis=0), 0)]
where the time goes in v2:
time: 394 us
  waiting for transfers between devices  220 us (56%)
  blocking collectives  96.9 us (25%)
  matrix products  29.2 us (7%)
  other arithmetic  17.8 us (5%)
  local copies, waits for them, and re-layouts  15.3 us (4%)
  between operations  14 us (4%)
    all_gather x1, waiting for transfers between devices, on_device(): every_slot = lax.all_gather(weights_low, ('x', 'z'), axis=0, tiled=True)  97.7 us
    all_to_all x1, blocking collectives, on_device(): arrived = lax.all_to_all(outgoing, 'x', 0, 0, tiled=True)  96.9 us
    psum x1, waiting for transfers between devices, gram_total(): return lax.psum(local_gram(values), 'own')  64.4 us
    reduce_scatter x1, waiting for transfers between devices, on_device(): gradient = lax.psum_scatter(row_sum, 'z', scatter_dimension=0, tiled=True)  58.3 us
    dot_general x13, matrix products, matmul(): jnp.einsum('srt,stu->sru', left, right, precision=lax.Precision.HIGHEST,...  19.5 us
    gather x1, local copies, waits for them, and re-layouts, on_device(): jnp.take(local_rows, source, axis=0)  8.62 us
  transfers between devices with their start and end apart: 3, of which 3 were waited for; matrix products, arithmetic and copies ran while one was open for 0% of the time, Pallas kernels for 0%

profile of v2, /device:TPU:1, one launch (start us, length us, event | category | flops | bytes accessed | tf_op | source)
XLA Modules:
  0.0 393.9 jit_solution(16766336314404221960)
XLA Ops:
  9.9 8.6 %gather_fusion = bf16[128,256,128]{2,1,0:T(8,128)(2,1)} fusion(bf16[64,256,128]{2,1,0:T(8,128)(2,1)} %bitcast.59, s32[1024]{0:T(1024)S(1)} %pad_clamp_fusion.1), kind=kCustom, calls=%fused_computation | custom fusion | bytes 16777728 | tf_op jit(solution)/shard_map/jit(_take)/gather | solution.py:90
  18.6 4.7 %select_select_fusion = bf16[4,32,256,128]{3,2,1,0:T(8,128)(2,1)S(1)} fusion(bf16[4,32,256,128]{3,2,1,0:T(8,128)(2,1)} %bitcast.58, pred[4,32]{1,0:T(4,128)(4,1)S(1)} %compare_and_fusion, pred[4,32]{1,0:T(4,128)(4,1)S(1)} %broadcast_in_dim.69), kind=kLoop, calls=%fused_computation.3 | loop fusion | flops 8388608 | bytes 16777472 | tf_op jit(solution)/shard_map/jit(_where)/select_n | solution.py:90
  23.2 96.9 %all_to_all.5 = bf16[4,32,256,128]{3,2,1,0:T(8,128)(2,1)S(1)} all-to-all(bf16[4,32,256,128]{3,2,1,0:T(8,128)(2,1)S(1)} %select_select_fusion), channel_id=1, replica_groups=mesh['x'=4,'z'=8,'own'=8] {'x'}, dimensions={0} | all-to-all | bytes 16777216 | tf_op jit(solution)/shard_map/all_to_all | solution.py:93
  120.1 3.6 convert_reduce_fusion
  123.8 58.3 %reduce-scatter.2.cloned.1.call-done = f32[4,256,128]{2,1,0:T(8,128)} async-done(((f32[32,256,128]{2,1,0:T(8,128)}), f32[4,256,128]{2,1,0:T(8,128)}) %reduce-scatter.2.cloned.1.call-update) | async-done | bytes 524304 | tf_op jit(solution)/shard_map/reduce_scatter | solution.py:95
  182.0 3.3 fusion.38
  185.6 64.4 %all-reduce.2.cloned.1.call-done = f32[4,256,256]{2,1,0:T(8,128)} async-done(((f32[4,256,256]{2,1,0:T(8,128)}), f32[4,256,256]{2,1,0:T(8,128)}) %all-reduce.2.cloned.1.call-update) | async-done | bytes 1048592 | tf_op jit(solution)/shard_map/psum | solution.py:51
  250.1 1.4 select_reduce_fusion
  251.5 3.4 fusion.4
  255.0 2.5 fusion.21
  257.4 1.2 fusion.19
  258.6 1.3 fusion.3
  259.9 1.2 fusion.17
  263.4 1.2 fusion.15
  264.6 1.3 fusion.2
  265.9 1.4 fusion.13
  269.6 1.3 fusion.1
  270.9 1.2 fusion.9
  273.1 1.2 fusion.7
  274.3 1.3 fusion
  275.6 2.0 fusion.45
  278.5 97.7 %all-gather.2.cloned.1.call-done = bf16[128,256,128]{2,1,0:T(8,128)(2,1)} async-done(((bf16[4,256,128]{2,1,0:T(8,128)(2,1)}), bf16[128,256,128]{2,1,0:T(8,128)(2,1)}) %all-gather.2.cloned.1.call-update) | async-done | bytes 8388624 | tf_op jit(solution)/shard_map/all_gather | solution.py:109
  376.2 6.5 %gather_fusion.1 = bf16[64,256,128]{2,1,0:T(8,128)(2,1)} fusion(bf16[128,256,128]{2,1,0:T(8,128)(2,1)} %all-gather.2.cloned.1.call-done, s32[1024]{0:T(1024)S(1)} %pad_clamp_fusion), kind=kCustom, calls=%fused_computation.1 | custom fusion | bytes 8388864 | tf_op jit(solution)/shard_map/jit(_take)/gather | solution.py:110
  382.7 4.6 %broadcast_select_fusion = bf16[64,256,128]{2,1,0:T(8,128)(2,1)} fusion(bf16[64,256,128]{2,1,0:T(8,128)(2,1)} %gather_fusion.1, pred[64]{0:T(512)(128)(4,1)S(1)} %get-tuple-element.3), kind=kLoop, calls=%fused_computation.4 | loop fusion | flops 2097152 | bytes 8388672 | tf_op jit(solution)/shard_map/jit(_take)/select_n | solution.py:110
  (36 shorter events, 9.6 us)
Async XLA Ops:
  7.2 174.9 %reduce-scatter.2.cloned.1.call-start = ((), (), s32[]{:S(2)}) async-start(), calls=%async_computation.2 | async-start | bytes 4718592 | tf_op jit(solution)/shard_map/reduce_scatter | solution.py:95
  120.1 61.9 %copy-start = (f32[1,4,256,128]{3,2,1,0:T(8,128)S(1)}, f32[1,4,256,128]{3,2,1,0:T(8,128)}, u32[]{:S(2)}) copy-start(f32[1,4,256,128]{3,2,1,0:T(8,128)} %param.6) | copy-start | bytes 1572868
  123.7 126.3 %all-reduce.2.cloned.1.call-start = ((), (), s32[]{:S(2)}) async-start(), calls=%async_computation.3 | async-start | bytes 2097152 | tf_op jit(solution)/shard_map/psum | solution.py:51
  185.3 190.9 %all-gather.2.cloned.1.call-start = ((), (), s32[]{:S(2)}) async-start(), calls=%async_computation.4 | async-start | bytes 8650752 | tf_op jit(solution)/shard_map/all_gather | solution.py:109
  185.6 75.5 %copy-start.1 = (f32[4,256,128]{2,1,0:T(8,128)S(1)}, f32[4,256,128]{2,1,0:T(8,128)}, u32[]{:S(2)}) copy-start(f32[4,256,128]{2,1,0:T(8,128)} %reduce-scatter.2.cloned.1.call-done) | copy-start | bytes 1572868
  269.6 6.1 %copy-start.2 = (f32[1,4,256,128]{3,2,1,0:T(8,128)S(1)}, f32[1,4,256,128]{3,2,1,0:T(8,128)}, u32[]{:S(2)}) copy-start(f32[1,4,256,128]{3,2,1,0:T(8,128)} %param.7) | copy-start | bytes 1572868
  270.8 6.8 %copy-start.3 = (s32[64,1]{0,1:T(1,128)S(1)}, s32[64,1]{0,1:T(1,128)}, u32[]{:S(2)}) copy-start(s32[64,1]{0,1:T(1,128)} %param.5) | copy-start | bytes 772
Sparse Core Ops, SparseCore 0:
  123.8 58.1 reduce-scatter.1
  185.5 64.5 all-reduce.1
  277.8 98.4 all-gather.1

commit v3 on v2

--- a/solution.py
+++ b/solution.py
@@ -47,8 +47,32 @@
     )
 
 
+def own_sum(total):
+    size = lax.axis_size("own")
+    index = lax.axis_index("own")
+    bits = []
+    bit = 1
+    while bit < size:
+        bits.append(bit)
+        bit *= 2
+    for bit in bits:
+        high = (index & bit) != 0
+        half = total.shape[1] // 2
+        lower, upper = total[:, :half], total[:, half:]
+        keep = jnp.where(high, upper, lower)
+        send = jnp.where(high, lower, upper)
+        pairs = [(i, i ^ bit) for i in range(size)]
+        total = keep + lax.ppermute(send, "own", pairs)
+    for bit in reversed(bits):
+        high = (index & bit) != 0
+        pairs = [(i, i ^ bit) for i in range(size)]
+        other = lax.ppermute(total, "own", pairs)
+        total = jnp.where(high, jnp.concatenate([other, total], axis=1), jnp.concatenate([total, other], axis=1))
+    return total
+
+
 def gram_total(values):
-    return lax.psum(local_gram(values), "own")
+    return own_sum(local_gram(values))
 
 
 def matmul(left, right):
@@ -101,8 +125,10 @@
     ortho = update * factor[:, None, None]
     gram = update_gram * (factor * factor)[:, None, None]
     eye = jnp.eye(block_rows, dtype=jnp.float32)[None]
-    for iteration in range(ITERS):
-        ortho, gram = newton_turn(ortho, gram, eye, iteration < ITERS - 1)
+    ortho, gram = lax.fori_loop(
+        0, ITERS - 1, lambda _, carry: newton_turn(*carry, eye, True), (ortho, gram)
+    )
+    ortho, gram = newton_turn(ortho, gram, eye, False)
     step_factor = STEP_SIZE * 0.2 * math.sqrt(max(block_rows, D))
     master_new = master[0] * (1.0 - STEP_SIZE * DECAY) - step_factor * ortho
     weights_low = master_new.astype(jnp.bfloat16)

time: 394 us -> 358 us (0.909)
  waiting for transfers between devices: 220 us -> 173 us
  starting transfers between devices: 0.3 us -> 13.7 us
    psum x1 -> x0, waiting for transfers between devices: 64.4 us -> none  [gram_total(): return lax.psum(local_gram(values), 'own')]
    ppermute x0 -> x6, waiting for transfers between devices: none -> 18.9 us  [the longest x3 10.4 us: own_sum(): total = keep + lax.ppermute(send, 'own', pairs)]
    ppermute x0 -> x6, starting transfers between devices: none -> 13.6 us  [the longest x3 8.68 us: own_sum(): other = lax.ppermute(total, 'own', pairs)]
  transfers between devices with their start and end apart: 3 -> 8, of which waited for: 3 -> 8; matrix products, arithmetic and copies ran while one was open for 0% -> 0% of each run, Pallas kernels for 0% -> 0%
where the time goes in v3:
time: 358 us
  waiting for transfers between devices  173 us (48%)
  blocking collectives  96.9 us (27%)
  matrix products  27.3 us (8%)
  other arithmetic  17.3 us (5%)
  local copies, waits for them, and re-layouts  15.4 us (4%)
  between operations  14.2 us (4%)
  starting transfers between devices  13.7 us (4%)
    all_to_all x1, blocking collectives, on_device(): arrived = lax.all_to_all(outgoing, 'x', 0, 0, tiled=True)  96.9 us
    all_gather x1, waiting for transfers between devices, on_device(): every_slot = lax.all_gather(weights_low, ('x', 'z'), axis=0, tiled=True)  95.9 us
    reduce_scatter x1, waiting for transfers between devices, on_device(): gradient = lax.psum_scatter(row_sum, 'z', scatter_dimension=0, tiled=True)  58.3 us
    dot_general x13, matrix products, matmul(): jnp.einsum('srt,stu->sru', left, right, precision=lax.Precision.HIGHEST,...  18.7 us
    ppermute x3, waiting for transfers between devices, own_sum(): total = keep + lax.ppermute(send, 'own', pairs)  10.4 us
    ppermute x3, starting transfers between devices, own_sum(): other = lax.ppermute(total, 'own', pairs)  8.68 us
    gather x1, local copies, waits for them, and re-layouts, on_device(): jnp.take(local_rows, source, axis=0)  8.62 us
    ppermute x3, waiting for transfers between devices, own_sum(): other = lax.ppermute(total, 'own', pairs)  8.49 us
  transfers between devices with their start and end apart: 8, of which 8 were waited for; matrix products, arithmetic and copies ran while one was open for 0% of the time, Pallas kernels for 0%

profile of v3, /device:TPU:1, one launch (start us, length us, event | category | flops | bytes accessed | tf_op | source)
XLA Modules:
  0.0 358.1 jit_solution(12086773051361824744)
XLA Ops:
  9.9 8.6 %gather_fusion = bf16[128,256,128]{2,1,0:T(8,128)(2,1)} fusion(bf16[64,256,128]{2,1,0:T(8,128)(2,1)} %bitcast.57, s32[1024]{0:T(1024)S(1)} %pad_clamp_fusion.1), kind=kCustom, calls=%fused_computation | custom fusion | bytes 16777728 | tf_op jit(solution)/shard_map/jit(_take)/gather | solution.py:114
  18.6 4.7 %select_select_fusion = bf16[4,32,256,128]{3,2,1,0:T(8,128)(2,1)S(1)} fusion(bf16[4,32,256,128]{3,2,1,0:T(8,128)(2,1)} %bitcast.56, pred[4,32]{1,0:T(4,128)(4,1)S(1)} %compare_and_fusion, pred[4,32]{1,0:T(4,128)(4,1)S(1)} %broadcast_in_dim.69), kind=kLoop, calls=%fused_computation.15 | loop fusion | flops 8388608 | bytes 16777472 | tf_op jit(solution)/shard_map/jit(_where)/select_n | solution.py:114
  23.2 96.9 %all_to_all.5 = bf16[4,32,256,128]{3,2,1,0:T(8,128)(2,1)S(1)} all-to-all(bf16[4,32,256,128]{3,2,1,0:T(8,128)(2,1)S(1)} %select_select_fusion), channel_id=1, replica_groups=mesh['x'=4,'z'=8,'own'=8] {'x'}, dimensions={0} | all-to-all | bytes 16777216 | tf_op jit(solution)/shard_map/all_to_all | solution.py:117
  120.1 3.6 %convert_reduce_fusion = f32[32,256,128]{2,1,0:T(8,128)} fusion(bf16[4,32,256,128]{3,2,1,0:T(8,128)(2,1)S(1)} %all_to_all.5), kind=kLoop, calls=%fused_computation.14 | loop fusion | flops 7340032 | bytes 12582912 | tf_op jit(solution)/shard_map/reduce_sum | solution.py:118
  123.8 58.3 %reduce-scatter.2.cloned.1.call-done = f32[4,256,128]{2,1,0:T(8,128)} async-done(((f32[32,256,128]{2,1,0:T(8,128)}), f32[4,256,128]{2,1,0:T(8,128)}) %reduce-scatter.2.cloned.1.call-update) | async-done | bytes 524304 | tf_op jit(solution)/shard_map/reduce_scatter | solution.py:119
  182.0 2.4 fusion.14
  185.3 1.5 collective-permute-done
  188.3 6.3 %collective-permute-done.1 = f32[4,64,256]{2,1,0:T(8,128)S(1)} collective-permute-done((f32[4,64,256]{2,1,0:T(8,128)S(1)}, f32[4,64,256]{2,1,0:T(8,128)S(1)}, u32[]{:S(2)}, u32[]{:S(2)}) %collective-permute-start.1) | collective-permute-done | bytes 262176 | tf_op jit(solution)/shard_map/ppermute | solution.py:65
  194.6 2.8 collective-permute-start.2
  197.5 2.6 collective-permute-done.2
  200.1 2.8 collective-permute-start.3
  202.9 2.6 collective-permute-done.3
  206.8 4.4 %collective-permute-done.4 = f32[4,64,256]{2,1,0:T(8,128)S(1)} collective-permute-done((f32[4,64,256]{2,1,0:T(8,128)S(1)}, f32[4,64,256]{2,1,0:T(8,128)S(1)}, u32[]{:S(2)}, u32[]{:S(2)}) %collective-permute-start.4) | collective-permute-done | bytes 262176 | tf_op jit(solution)/shard_map/ppermute | solution.py:69
  211.3 4.5 %collective-permute-start.5 = (f32[4,128,256]{2,1,0:T(8,128)S(1)}, f32[4,128,256]{2,1,0:T(8,128)S(1)}, u32[]{:S(2)}, u32[]{:S(2)}) collective-permute-start(f32[4,128,256]{2,1,0:T(8,128)S(1)} %maximum_select_fusion.1), channel_id=1, source_target_pairs={{0,1},{1,0},{2,3},{3,2},{4,5},{5,4},{6,7},{7,6},{8,9},{9,8},{10,11... | collective-permute-start | bytes 1572872 | tf_op jit(solution)/shard_map/ppermute | solution.py:69
  215.8 1.5 collective-permute-done.5
  218.8 22.1 %while.13 = (s32[]{:T(128)}, f32[4,256,128]{2,1,0:T(8,128)S(1)}, f32[4,256,256]{2,1,0:T(8,128)S(1)}, s32[]{:T(128)}) while((s32[]{:T(128)}, f32[4,256,128]{2,1,0:T(8,128)S(1)}, f32[4,256,256]{2,1,0:T(8,128)S(1)}, s32[]{:T(128)}) %tuple.29), condition=%wide.region_8.9_spmd.clone, body=%wide.region_7.8_spmd.clone.sunk | while | flops 2820276224 | bytes 12320821 | solution.py:128
  220.1 1.9 fusion.51
  225.6 1.9 fusion.51
  231.2 1.9 fusion.51
  236.7 1.9 fusion.51
  242.2 2.0 fusion.20
  244.3 95.9 %all-gather.2.cloned.1.call-done = bf16[128,256,128]{2,1,0:T(8,128)(2,1)} async-done(((bf16[4,256,128]{2,1,0:T(8,128)(2,1)}), bf16[128,256,128]{2,1,0:T(8,128)(2,1)}) %all-gather.2.cloned.1.call-update) | async-done | bytes 8388624 | tf_op jit(solution)/shard_map/all_gather | solution.py:135
  340.1 6.5 %gather_fusion.1 = bf16[64,256,128]{2,1,0:T(8,128)(2,1)} fusion(bf16[128,256,128]{2,1,0:T(8,128)(2,1)} %all-gather.2.cloned.1.call-done, s32[1024]{0:T(1024)S(1)} %pad_clamp_fusion), kind=kCustom, calls=%fused_computation.1 | custom fusion | bytes 8388864 | tf_op jit(solution)/shard_map/jit(_take)/gather | solution.py:136
  346.6 4.6 %broadcast_select_fusion = bf16[64,256,128]{2,1,0:T(8,128)(2,1)} fusion(bf16[64,256,128]{2,1,0:T(8,128)(2,1)} %gather_fusion.1, pred[64]{0:T(512)(128)(4,1)S(1)} %get-tuple-element.42), kind=kLoop, calls=%fused_computation.16 | loop fusion | flops 2097152 | bytes 8388672 | tf_op jit(solution)/shard_map/jit(_take)/select_n | solution.py:136
  (62 shorter events, 23.6 us)
Async XLA Ops:
  7.2 174.9 %reduce-scatter.2.cloned.1.call-start = ((), (), s32[]{:S(2)}) async-start(), calls=%async_computation.2 | async-start | bytes 4718592 | tf_op jit(solution)/shard_map/reduce_scatter | solution.py:119
  120.1 61.9 %copy-start = (f32[1,4,256,128]{3,2,1,0:T(8,128)S(1)}, f32[1,4,256,128]{3,2,1,0:T(8,128)}, u32[]{:S(2)}) copy-start(f32[1,4,256,128]{3,2,1,0:T(8,128)} %param.8) | copy-start | bytes 1572868
  123.7 216.4 %all-gather.2.cloned.1.call-start = ((), (), s32[]{:S(2)}) async-start(), calls=%async_computation.3 | async-start | bytes 8650752 | tf_op jit(solution)/shard_map/all_gather | solution.py:135
  182.0 35.8 %copy-start.1 = (f32[4,256,128]{2,1,0:T(8,128)S(1)}, f32[4,256,128]{2,1,0:T(8,128)}, u32[]{:S(2)}) copy-start(f32[4,256,128]{2,1,0:T(8,128)} %reduce-scatter.2.cloned.1.call-done) | copy-start | bytes 1572868
  184.5 2.4 collective-permute-start
  187.0 7.6 %collective-permute-start.1 = (f32[4,64,256]{2,1,0:T(8,128)S(1)}, f32[4,64,256]{2,1,0:T(8,128)S(1)}, u32[]{:S(2)}, u32[]{:S(2)}) collective-permute-start(f32[4,64,256]{2,1,0:T(8,128)S(1)} %slice_select_fusion.1), channel_id=1, source_target_pairs={{0,2},{1,3},{2,0},{3,1},{4,6},{5,7},{6,4},{7,5},{8,10},{9,11},{10,... | collective-permute-start | bytes 786440 | tf_op jit(solution)/shard_map/ppermute | solution.py:65
  194.6 5.4 %collective-permute-start.2 = (f32[4,32,256]{2,1,0:T(8,128)S(1)}, f32[4,32,256]{2,1,0:T(8,128)S(1)}, u32[]{:S(2)}, u32[]{:S(2)}) collective-permute-start(f32[4,32,256]{2,1,0:T(8,128)S(1)} %slice_select_fusion.2), channel_id=1, source_target_pairs={{0,4},{1,5},{2,6},{3,7},{4,0},{5,1},{6,2},{7,3},{8,12},{9,13},{10,... | collective-permute-start | bytes 393224 | tf_op jit(solution)/shard_map/ppermute | solution.py:65
  200.1 5.4 %collective-permute-start.3 = (f32[4,32,256]{2,1,0:T(8,128)S(1)}, f32[4,32,256]{2,1,0:T(8,128)S(1)}, u32[]{:S(2)}, u32[]{:S(2)}) collective-permute-start(f32[4,32,256]{2,1,0:T(8,128)S(1)} %select_add_fusion.2), channel_id=1, source_target_pairs={{0,4},{1,5},{2,6},{3,7},{4,0},{5,1},{6,2},{7,3},{8,12},{9,13},{10,... | collective-permute-start | bytes 393224 | tf_op jit(solution)/shard_map/ppermute | solution.py:69
  205.5 5.7 %collective-permute-start.4 = (f32[4,64,256]{2,1,0:T(8,128)S(1)}, f32[4,64,256]{2,1,0:T(8,128)S(1)}, u32[]{:S(2)}, u32[]{:S(2)}) collective-permute-start(f32[4,64,256]{2,1,0:T(8,128)S(1)} %maximum_select_fusion.2), channel_id=1, source_target_pairs={{0,2},{1,3},{2,0},{3,1},{4,6},{5,7},{6,4},{7,5},{8,10},{9,11},{10,... | collective-permute-start | bytes 786440 | tf_op jit(solution)/shard_map/ppermute | solution.py:69
  211.3 6.1 %collective-permute-start.5 = (f32[4,128,256]{2,1,0:T(8,128)S(1)}, f32[4,128,256]{2,1,0:T(8,128)S(1)}, u32[]{:S(2)}, u32[]{:S(2)}) collective-permute-start(f32[4,128,256]{2,1,0:T(8,128)S(1)} %maximum_select_fusion.1), channel_id=1, source_target_pairs={{0,1},{1,0},{2,3},{3,2},{4,5},{5,4},{6,7},{7,6},{8,9},{9,8},{10,11... | collective-permute-start | bytes 1572872 | tf_op jit(solution)/shard_map/ppermute | solution.py:69
  218.8 23.4 %copy-start.2 = (f32[1,4,256,128]{3,2,1,0:T(8,128)S(1)}, f32[1,4,256,128]{3,2,1,0:T(8,128)}, u32[]{:S(2)}) copy-start(f32[1,4,256,128]{3,2,1,0:T(8,128)} %param.9) | copy-start | bytes 1572868
  218.8 25.4 %copy-start.3 = (s32[64,1]{0,1:T(1,128)S(1)}, s32[64,1]{0,1:T(1,128)}, u32[]{:S(2)}) copy-start(s32[64,1]{0,1:T(1,128)} %param.7) | copy-start | bytes 772
Sparse Core Ops, SparseCore 0:
  123.8 58.1 reduce-scatter.1
  244.3 95.7 all-gather.1

commit v4 on v3

--- a/solution.py
+++ b/solution.py
@@ -113,10 +113,13 @@
     present, source = slot_sources(target, group_count * slot_count, block_count)
     outgoing = jnp.where(present[:, None, None], jnp.take(local_rows, source, axis=0), 0)
     row_count = lax.axis_size("x")
-    outgoing = outgoing.reshape((row_count, -1) + outgoing.shape[1:])
-    arrived = lax.all_to_all(outgoing, "x", 0, 0, tiled=True)
-    row_sum = jnp.sum(arrived.astype(jnp.float32), axis=0)
-    gradient = lax.psum_scatter(row_sum, "z", scatter_dimension=0, tiled=True)
+    outgoing = outgoing.reshape((row_count, -1, slot_count) + outgoing.shape[1:])
+    pieces = []
+    for slot in range(slot_count):
+        arrived = lax.all_to_all(outgoing[:, :, slot], "x", 0, 0, tiled=True)
+        row_sum = jnp.sum(arrived.astype(jnp.float32), axis=0)
+        pieces.append(lax.psum_scatter(row_sum, "z", scatter_dimension=0, tiled=True))
+    gradient = jnp.concatenate(pieces, axis=0)
     momentum_new = BETA * momentum[0] + gradient
     update = gradient + BETA * momentum_new
     update_gram = gram_total(update)

time: 358 us -> 395 us (1.10)
  blocking collectives: 96.9 us -> 110 us
  waiting for transfers between devices: 173 us -> 184 us
  local copies, waits for them, and re-layouts: 15.4 us -> 21.7 us
  starting transfers between devices: 13.7 us -> 18.6 us
    all_to_all x1 -> x4, blocking collectives: 96.9 us -> 110 us  [on_device(): arrived = lax.all_to_all(outgoing[:, :, slot], 'x', 0, 0, tiled=True)]
    reduce_scatter x1 -> x4, waiting for transfers between devices: 58.3 us -> 70.3 us  [on_device(): lax.psum_scatter(row_sum, 'z', scatter_dimension=0, tiled=True)]
    ppermute x3, starting transfers between devices: 4.95 us -> 9.78 us  [own_sum(): total = keep + lax.ppermute(send, 'own', pairs)]
  transfers between devices with their start and end apart: 8 -> 11, of which waited for: 8 -> 9; matrix products, arithmetic and copies ran while one was open for 0% -> 2% of each run, Pallas kernels for 0% -> 0%
where the time goes in v4:
time: 395 us; the launch traced here: 394 us
  waiting for transfers between devices  184 us (47%)
  blocking collectives  110 us (28%)
  matrix products  26 us (7%)
  local copies, waits for them, and re-layouts  21.7 us (5%)
  other arithmetic  19.1 us (5%)
  starting transfers between devices  18.6 us (5%)
  between operations  14.1 us (4%)
    all_to_all x4, blocking collectives, on_device(): arrived = lax.all_to_all(outgoing[:, :, slot], 'x', 0, 0, tiled=True)  110 us
    all_gather x1, waiting for transfers between devices, on_device(): every_slot = lax.all_gather(weights_low, ('x', 'z'), axis=0, tiled=True)  95 us
    reduce_scatter x4, waiting for transfers between devices, on_device(): lax.psum_scatter(row_sum, 'z', scatter_dimension=0, tiled=True)  70.3 us
    dot_general x13, matrix products, matmul(): jnp.einsum('srt,stu->sru', left, right, precision=lax.Precision.HIGHEST,...  18.7 us
    ppermute x3, waiting for transfers between devices, own_sum(): total = keep + lax.ppermute(send, 'own', pairs)  10.4 us
    ppermute x3, starting transfers between devices, own_sum(): total = keep + lax.ppermute(send, 'own', pairs)  9.78 us
    gather x1, local copies, waits for them, and re-layouts, on_device(): jnp.take(local_rows, source, axis=0)  8.64 us
    ppermute x3, waiting for transfers between devices, own_sum(): other = lax.ppermute(total, 'own', pairs)  8.6 us
  transfers between devices with their start and end apart: 11, of which 9 were waited for; matrix products, arithmetic and copies ran while one was open for 2% of the time, Pallas kernels for 0%

profile of v4, /device:TPU:1, one launch (start us, length us, event | category | flops | bytes accessed | tf_op | source)
XLA Modules:
  0.0 394.3 jit_solution(7504612823183251551)
XLA Ops:
  10.0 8.6 %gather_fusion = bf16[128,256,128]{2,1,0:T(8,128)(2,1)} fusion(bf16[64,256,128]{2,1,0:T(8,128)(2,1)} %bitcast.67, s32[1024]{0:T(1024)S(1)} %pad_clamp_fusion.1), kind=kCustom, calls=%fused_computation | custom fusion | bytes 16777728 | tf_op jit(solution)/shard_map/jit(_take)/gather | solution.py:114
  18.6 4.7 %select_select_fusion = bf16[4,8,4,256,128]{4,3,2,1,0:T(8,128)(2,1)S(1)} fusion(bf16[4,8,4,256,128]{4,3,2,1,0:T(8,128)(2,1)} %bitcast.66, pred[4,8,4]{2,1,0:T(8,128)(4,1)S(1)} %compare_and_fusion, pred[4,8,4]{2,1,0:T(8,128)(4,1)S(1)} %broadcast_in_dim.67), kind=kLoop, calls=%fused_computation.14 | loop fusion | flops 8388608 | bytes 16777472 | tf_op jit(solution)/shard_map/jit(_where)/select_n | solution.py:114
  23.3 2.5 slice_bitcast_fusion.3
  25.8 30.0 %all_to_all.20 = bf16[4,8,256,128]{3,2,1,0:T(8,128)(2,1)S(1)} all-to-all(bf16[4,8,256,128]{3,2,1,0:T(8,128)(2,1)S(1)} %get-tuple-element.46), channel_id=1, replica_groups=mesh['x'=4,'z'=8,'own'=8] {'x'}, dimensions={0} | all-to-all | bytes 4194304 | tf_op jit(solution)/shard_map/all_to_all | solution.py:119
  57.2 28.1 %all_to_all.21 = bf16[4,8,256,128]{3,2,1,0:T(8,128)(2,1)S(1)} all-to-all(bf16[4,8,256,128]{3,2,1,0:T(8,128)(2,1)} %get-tuple-element.49), channel_id=1, replica_groups=mesh['x'=4,'z'=8,'own'=8] {'x'}, dimensions={0} | all-to-all | bytes 4194304 | tf_op jit(solution)/shard_map/all_to_all | solution.py:119
  86.7 27.0 %all_to_all.22 = bf16[4,8,256,128]{3,2,1,0:T(8,128)(2,1)S(1)} all-to-all(bf16[4,8,256,128]{3,2,1,0:T(8,128)(2,1)} %get-tuple-element.48), channel_id=1, replica_groups=mesh['x'=4,'z'=8,'own'=8] {'x'}, dimensions={0} | all-to-all | bytes 4194304 | tf_op jit(solution)/shard_map/all_to_all | solution.py:119
  115.2 25.1 %all_to_all.23 = bf16[4,8,256,128]{3,2,1,0:T(8,128)(2,1)S(1)} all-to-all(bf16[4,8,256,128]{3,2,1,0:T(8,128)(2,1)S(1)} %get-tuple-element.47), channel_id=1, replica_groups=mesh['x'=4,'z'=8,'own'=8] {'x'}, dimensions={0} | all-to-all | bytes 4194304 | tf_op jit(solution)/shard_map/all_to_all | solution.py:119
  143.5 30.6 %reduce-scatter.9.cloned.1.call-done = f32[1,256,128]{2,1,0:T(8,128)} async-done(((f32[8,256,128]{2,1,0:T(8,128)}), f32[1,256,128]{2,1,0:T(8,128)}) %reduce-scatter.9.cloned.1.call-update) | async-done | bytes 131088 | tf_op jit(solution)/shard_map/reduce_scatter | solution.py:121
  175.0 39.7 %reduce-scatter.11.cloned.1.call-done = f32[1,256,128]{2,1,0:T(8,128)} async-done(((f32[8,256,128]{2,1,0:T(8,128)}), f32[1,256,128]{2,1,0:T(8,128)}) %reduce-scatter.11.cloned.1.call-update) | async-done | bytes 131088 | tf_op jit(solution)/shard_map/reduce_scatter | solution.py:121
  216.8 5.7 %collective-permute-start = (f32[4,128,256]{2,1,0:T(8,128)S(1)}, f32[4,128,256]{2,1,0:T(8,128)S(1)}, u32[]{:S(2)}, u32[]{:S(2)}) collective-permute-start(f32[4,128,256]{2,1,0:T(8,128)S(1)} %slice_select_fusion), channel_id=1, source_target_pairs={{0,1},{1,0},{2,3},{3,2},{4,5},{5,4},{6,7},{7,6},{8,9},{9,8},{10,11... | collective-permute-start | bytes 1572872 | tf_op jit(solution)/shard_map/ppermute | solution.py:65
  225.5 6.3 %collective-permute-done.1 = f32[4,64,256]{2,1,0:T(8,128)S(1)} collective-permute-done((f32[4,64,256]{2,1,0:T(8,128)S(1)}, f32[4,64,256]{2,1,0:T(8,128)S(1)}, u32[]{:S(2)}, u32[]{:S(2)}) %collective-permute-start.1) | collective-permute-done | bytes 262176 | tf_op jit(solution)/shard_map/ppermute | solution.py:65
  231.9 2.8 collective-permute-start.2
  234.7 2.6 collective-permute-done.2
  237.3 2.8 collective-permute-start.3
  240.2 2.6 collective-permute-done.3
  244.0 4.5 %collective-permute-done.4 = f32[4,64,256]{2,1,0:T(8,128)S(1)} collective-permute-done((f32[4,64,256]{2,1,0:T(8,128)S(1)}, f32[4,64,256]{2,1,0:T(8,128)S(1)}, u32[]{:S(2)}, u32[]{:S(2)}) %collective-permute-start.4) | collective-permute-done | bytes 262176 | tf_op jit(solution)/shard_map/ppermute | solution.py:69
  248.6 4.5 %collective-permute-start.5 = (f32[4,128,256]{2,1,0:T(8,128)S(1)}, f32[4,128,256]{2,1,0:T(8,128)S(1)}, u32[]{:S(2)}, u32[]{:S(2)}) collective-permute-start(f32[4,128,256]{2,1,0:T(8,128)S(1)} %maximum_select_fusion.1), channel_id=1, source_target_pairs={{0,1},{1,0},{2,3},{3,2},{4,5},{5,4},{6,7},{7,6},{8,9},{9,8},{10,11... | collective-permute-start | bytes 1572872 | tf_op jit(solution)/shard_map/ppermute | solution.py:69
  255.3 22.1 %while.13 = (s32[]{:T(128)}, f32[4,256,128]{2,1,0:T(8,128)S(1)}, f32[4,256,256]{2,1,0:T(8,128)S(1)}, s32[]{:T(128)}) while((s32[]{:T(128)}, f32[4,256,128]{2,1,0:T(8,128)S(1)}, f32[4,256,256]{2,1,0:T(8,128)S(1)}, s32[]{:T(128)}) %tuple.31), condition=%wide.region_14.15_spmd.clone, body=%wide.region_13.14_spmd.clone.sunk | while | flops 2820276224 | bytes 12320821 | solution.py:131
  262.1 1.9 fusion.53
  267.6 1.9 fusion.53
  278.7 2.0 fusion.22
  281.7 95.0 %all-gather.2.cloned.1.call-done = bf16[128,256,128]{2,1,0:T(8,128)(2,1)} async-done(((bf16[4,256,128]{2,1,0:T(8,128)(2,1)}), bf16[128,256,128]{2,1,0:T(8,128)(2,1)}) %all-gather.2.cloned.1.call-update) | async-done | bytes 8388624 | tf_op jit(solution)/shard_map/all_gather | solution.py:138
  376.7 6.5 %gather_fusion.1 = bf16[64,256,128]{2,1,0:T(8,128)(2,1)} fusion(bf16[128,256,128]{2,1,0:T(8,128)(2,1)} %all-gather.2.cloned.1.call-done, s32[1024]{0:T(1024)S(1)} %pad_clamp_fusion), kind=kCustom, calls=%fused_computation.1 | custom fusion | bytes 8388864 | tf_op jit(solution)/shard_map/jit(_take)/gather | solution.py:139
  383.1 4.6 %broadcast_select_fusion = bf16[64,256,128]{2,1,0:T(8,128)(2,1)} fusion(bf16[64,256,128]{2,1,0:T(8,128)(2,1)} %gather_fusion.1, pred[64]{0:T(512)(128)(4,1)S(1)} %get-tuple-element.42), kind=kLoop, calls=%fused_computation.19 | loop fusion | flops 2097152 | bytes 8388672 | tf_op jit(solution)/shard_map/jit(_take)/select_n | solution.py:139
  (89 shorter events, 39.9 us)
Async XLA Ops:
  7.2 134.5 %reduce-scatter.5.cloned.1.call-start = ((), (), s32[]{:S(2)}) async-start(), calls=%async_computation.8 | async-start | bytes 1179648 | tf_op jit(solution)/shard_map/reduce_scatter | solution.py:121
  57.2 85.5 %reduce-scatter.7.cloned.1.call-start = ((), (), s32[]{:S(2)}) async-start(), calls=%async_computation.9 | async-start | bytes 1179648 | tf_op jit(solution)/shard_map/reduce_scatter | solution.py:121
  86.7 87.4 %reduce-scatter.9.cloned.1.call-start = ((), (), s32[]{:S(2)}) async-start(), calls=%async_computation.10 | async-start | bytes 1179648 | tf_op jit(solution)/shard_map/reduce_scatter | solution.py:121
  115.1 99.6 %reduce-scatter.11.cloned.1.call-start = ((), (), s32[]{:S(2)}) async-start(), calls=%async_computation.11 | async-start | bytes 1179648 | tf_op jit(solution)/shard_map/reduce_scatter | solution.py:121
  115.1 100.5 %copy-start = (f32[1,4,256,128]{3,2,1,0:T(8,128)S(1)}, f32[1,4,256,128]{3,2,1,0:T(8,128)}, u32[]{:S(2)}) copy-start(f32[1,4,256,128]{3,2,1,0:T(8,128)} %param.8) | copy-start | bytes 1572868
  141.6 235.1 %all-gather.2.cloned.1.call-start = ((), (), s32[]{:S(2)}) async-start(), calls=%async_computation.12 | async-start | bytes 8650752 | tf_op jit(solution)/shard_map/all_gather | solution.py:138
  216.8 7.2 %collective-permute-start = (f32[4,128,256]{2,1,0:T(8,128)S(1)}, f32[4,128,256]{2,1,0:T(8,128)S(1)}, u32[]{:S(2)}, u32[]{:S(2)}) collective-permute-start(f32[4,128,256]{2,1,0:T(8,128)S(1)} %slice_select_fusion), channel_id=1, source_target_pairs={{0,1},{1,0},{2,3},{3,2},{4,5},{5,4},{6,7},{7,6},{8,9},{9,8},{10,11... | collective-permute-start | bytes 1572872 | tf_op jit(solution)/shard_map/ppermute | solution.py:65
  224.2 7.6 %collective-permute-start.1 = (f32[4,64,256]{2,1,0:T(8,128)S(1)}, f32[4,64,256]{2,1,0:T(8,128)S(1)}, u32[]{:S(2)}, u32[]{:S(2)}) collective-permute-start(f32[4,64,256]{2,1,0:T(8,128)S(1)} %slice_select_fusion.1), channel_id=1, source_target_pairs={{0,2},{1,3},{2,0},{3,1},{4,6},{5,7},{6,4},{7,5},{8,10},{9,11},{10,... | collective-permute-start | bytes 786440 | tf_op jit(solution)/shard_map/ppermute | solution.py:65
  231.9 5.4 %collective-permute-start.2 = (f32[4,32,256]{2,1,0:T(8,128)S(1)}, f32[4,32,256]{2,1,0:T(8,128)S(1)}, u32[]{:S(2)}, u32[]{:S(2)}) collective-permute-start(f32[4,32,256]{2,1,0:T(8,128)S(1)} %slice_select_fusion.2), channel_id=1, source_target_pairs={{0,4},{1,5},{2,6},{3,7},{4,0},{5,1},{6,2},{7,3},{8,12},{9,13},{10,... | collective-permute-start | bytes 393224 | tf_op jit(solution)/shard_map/ppermute | solution.py:65
  237.3 5.4 %collective-permute-start.3 = (f32[4,32,256]{2,1,0:T(8,128)S(1)}, f32[4,32,256]{2,1,0:T(8,128)S(1)}, u32[]{:S(2)}, u32[]{:S(2)}) collective-permute-start(f32[4,32,256]{2,1,0:T(8,128)S(1)} %select_add_fusion.2), channel_id=1, source_target_pairs={{0,4},{1,5},{2,6},{3,7},{4,0},{5,1},{6,2},{7,3},{8,12},{9,13},{10,... | collective-permute-start | bytes 393224 | tf_op jit(solution)/shard_map/ppermute | solution.py:69
  242.8 5.8 %collective-permute-start.4 = (f32[4,64,256]{2,1,0:T(8,128)S(1)}, f32[4,64,256]{2,1,0:T(8,128)S(1)}, u32[]{:S(2)}, u32[]{:S(2)}) collective-permute-start(f32[4,64,256]{2,1,0:T(8,128)S(1)} %maximum_select_fusion.2), channel_id=1, source_target_pairs={{0,2},{1,3},{2,0},{3,1},{4,6},{5,7},{6,4},{7,5},{8,10},{9,11},{10,... | collective-permute-start | bytes 786440 | tf_op jit(solution)/shard_map/ppermute | solution.py:69
  248.6 6.0 %collective-permute-start.5 = (f32[4,128,256]{2,1,0:T(8,128)S(1)}, f32[4,128,256]{2,1,0:T(8,128)S(1)}, u32[]{:S(2)}, u32[]{:S(2)}) collective-permute-start(f32[4,128,256]{2,1,0:T(8,128)S(1)} %maximum_select_fusion.1), channel_id=1, source_target_pairs={{0,1},{1,0},{2,3},{3,2},{4,5},{5,4},{6,7},{7,6},{8,9},{9,8},{10,11... | collective-permute-start | bytes 1572872 | tf_op jit(solution)/shard_map/ppermute | solution.py:69
  255.2 23.5 %copy-start.5 = (f32[1,4,256,128]{3,2,1,0:T(8,128)S(1)}, f32[1,4,256,128]{3,2,1,0:T(8,128)}, u32[]{:S(2)}) copy-start(f32[1,4,256,128]{3,2,1,0:T(8,128)} %param.9) | copy-start | bytes 1572868
  277.4 3.3 copy-start.6
  277.4 3.4 copy-start.1
  277.4 3.4 copy-start.2
  277.4 3.4 copy-start.3
  277.5 3.4 copy-start.4
Sparse Core Ops, SparseCore 0:
  57.3 37.2 reduce-scatter.4
  97.1 37.5 reduce-scatter.6
  137.2 36.8 reduce-scatter.8
  177.1 37.6 reduce-scatter.10
  280.9 95.7 all-gather.1

commit v5 on v3

--- a/solution.py
+++ b/solution.py
@@ -111,7 +111,7 @@
     owner_list = owner[:, 0]
     target = slot_targets(owner_list, group_count, slot_count)
     present, source = slot_sources(target, group_count * slot_count, block_count)
-    outgoing = jnp.where(present[:, None, None], jnp.take(local_rows, source, axis=0), 0)
+    outgoing = jnp.where(present[:, None, None], jnp.take(local_rows, source, axis=0, mode="clip"), 0)
     row_count = lax.axis_size("x")
     outgoing = outgoing.reshape((row_count, -1) + outgoing.shape[1:])
     arrived = lax.all_to_all(outgoing, "x", 0, 0, tiled=True)
@@ -132,8 +132,9 @@
     step_factor = STEP_SIZE * 0.2 * math.sqrt(max(block_rows, D))
     master_new = master[0] * (1.0 - STEP_SIZE * DECAY) - step_factor * ortho
     weights_low = master_new.astype(jnp.bfloat16)
-    every_slot = lax.all_gather(weights_low, ("x", "z"), axis=0, tiled=True)
-    weights = jnp.take(every_slot, target, axis=0)
+    column = lax.all_gather(weights_low, "z", axis=0, tiled=True)
+    every_slot = lax.all_gather(column, "x", axis=0, tiled=True)
+    weights = jnp.take(every_slot, target, axis=0, mode="clip")
     return (momentum_new[None], master_new[None], weights)
 
 

time: 358 us -> 386 us (1.078)
  waiting for transfers between devices: 173 us -> 204 us
    all_gather x1 -> x2, waiting for transfers between devices: 95.9 us -> 125 us  [the longest x1 90 us: on_device(): every_slot = lax.all_gather(column, 'x', axis=0, tiled=True)]
    select_n x3 -> x1, other arithmetic: 9.31 us -> 7.24 us  [on_device(): jnp.where(present[:, None, None], jnp.take(local_rows, source, axis=0, mo...]
  transfers between devices with their start and end apart: 8 -> 9, of which waited for: 8 -> 9; matrix products, arithmetic and copies ran while one was open for 0% -> 0% of each run, Pallas kernels for 0% -> 0%
where the time goes in v5:
time: 386 us
  waiting for transfers between devices  204 us (53%)
  blocking collectives  96.2 us (25%)
  matrix products  27.3 us (7%)
  local copies, waits for them, and re-layouts  15.4 us (4%)
  other arithmetic  15.2 us (4%)
  between operations  13.9 us (4%)
  starting transfers between devices  13.7 us (4%)
    all_to_all x1, blocking collectives, on_device(): arrived = lax.all_to_all(outgoing, 'x', 0, 0, tiled=True)  96.2 us
    all_gather x1, waiting for transfers between devices, on_device(): every_slot = lax.all_gather(column, 'x', axis=0, tiled=True)  90 us
    reduce_scatter x1, waiting for transfers between devices, on_device(): gradient = lax.psum_scatter(row_sum, 'z', scatter_dimension=0, tiled=True)  59.3 us
    all_gather x1, waiting for transfers between devices, on_device(): column = lax.all_gather(weights_low, 'z', axis=0, tiled=True)  35.5 us
    dot_general x13, matrix products, matmul(): jnp.einsum('srt,stu->sru', left, right, precision=lax.Precision.HIGHEST,...  18.7 us
    ppermute x3, waiting for transfers between devices, own_sum(): total = keep + lax.ppermute(send, 'own', pairs)  10.4 us
    ppermute x3, starting transfers between devices, own_sum(): other = lax.ppermute(total, 'own', pairs)  8.67 us
    gather x1, local copies, waits for them, and re-layouts, on_device(): jnp.take(local_rows, source, axis=0, mode='clip')  8.63 us
  transfers between devices with their start and end apart: 9, of which 9 were waited for; matrix products, arithmetic and copies ran while one was open for 0% of the time, Pallas kernels for 0%

profile of v5, /device:TPU:1, one launch (start us, length us, event | category | flops | bytes accessed | tf_op | source)
XLA Modules:
  0.0 385.5 jit_solution(14429518743541629824)
XLA Ops:
  9.8 8.6 %gather_fusion = bf16[128,256,128]{2,1,0:T(8,128)(2,1)} fusion(bf16[64,256,128]{2,1,0:T(8,128)(2,1)} %bitcast.51, s32[1024]{0:T(1024)S(1)} %pad_clamp_fusion.1), kind=kCustom, calls=%fused_computation | custom fusion | bytes 16777728 | tf_op jit(solution)/shard_map/jit(_take)/gather | solution.py:114
  18.5 7.2 %broadcast_select_fusion = bf16[4,32,256,128]{3,2,1,0:T(8,128)(2,1)} fusion(bf16[4,32,256,128]{3,2,1,0:T(8,128)(2,1)} %bitcast.50, pred[4,32]{1,0:T(4,128)(4,1)S(1)} %broadcast_in_dim.55), kind=kLoop, calls=%fused_computation.15 | loop fusion | flops 4194304 | bytes 16777344 | tf_op jit(solution)/shard_map/jit(_where)/select_n | solution.py:114
  25.7 96.2 %all_to_all.5 = bf16[4,32,256,128]{3,2,1,0:T(8,128)(2,1)S(1)} all-to-all(bf16[4,32,256,128]{3,2,1,0:T(8,128)(2,1)} %broadcast_select_fusion), channel_id=1, replica_groups=mesh['x'=4,'z'=8,'own'=8] {'x'}, dimensions={0} | all-to-all | bytes 16777216 | tf_op jit(solution)/shard_map/all_to_all | solution.py:117
  121.9 3.6 convert_reduce_fusion
  125.5 59.3 %reduce-scatter.2.cloned.1.call-done = f32[4,256,128]{2,1,0:T(8,128)} async-done(((f32[32,256,128]{2,1,0:T(8,128)}), f32[4,256,128]{2,1,0:T(8,128)}) %reduce-scatter.2.cloned.1.call-update) | async-done | bytes 524304 | tf_op jit(solution)/shard_map/reduce_scatter | solution.py:119
  184.8 2.4 fusion.14
  188.1 1.5 collective-permute-done
  191.1 6.3 %collective-permute-done.1 = f32[4,64,256]{2,1,0:T(8,128)S(1)} collective-permute-done((f32[4,64,256]{2,1,0:T(8,128)S(1)}, f32[4,64,256]{2,1,0:T(8,128)S(1)}, u32[]{:S(2)}, u32[]{:S(2)}) %collective-permute-start.1) | collective-permute-done | bytes 262176 | tf_op jit(solution)/shard_map/ppermute | solution.py:65
  197.4 2.8 collective-permute-start.2
  200.3 2.6 collective-permute-done.2
  202.9 2.8 collective-permute-start.3
  205.7 2.6 collective-permute-done.3
  209.6 4.4 %collective-permute-done.4 = f32[4,64,256]{2,1,0:T(8,128)S(1)} collective-permute-done((f32[4,64,256]{2,1,0:T(8,128)S(1)}, f32[4,64,256]{2,1,0:T(8,128)S(1)}, u32[]{:S(2)}, u32[]{:S(2)}) %collective-permute-start.4) | collective-permute-done | bytes 262176 | tf_op jit(solution)/shard_map/ppermute | solution.py:69
  214.1 4.5 %collective-permute-start.5 = (f32[4,128,256]{2,1,0:T(8,128)S(1)}, f32[4,128,256]{2,1,0:T(8,128)S(1)}, u32[]{:S(2)}, u32[]{:S(2)}) collective-permute-start(f32[4,128,256]{2,1,0:T(8,128)S(1)} %maximum_select_fusion.1), channel_id=1, source_target_pairs={{0,1},{1,0},{2,3},{3,2},{4,5},{5,4},{6,7},{7,6},{8,9},{9,8},{10,11... | collective-permute-start | bytes 1572872 | tf_op jit(solution)/shard_map/ppermute | solution.py:69
  218.6 1.5 collective-permute-done.5
  221.6 22.1 %while.13 = (s32[]{:T(128)}, f32[4,256,128]{2,1,0:T(8,128)S(1)}, f32[4,256,256]{2,1,0:T(8,128)S(1)}, s32[]{:T(128)}) while((s32[]{:T(128)}, f32[4,256,128]{2,1,0:T(8,128)S(1)}, f32[4,256,256]{2,1,0:T(8,128)S(1)}, s32[]{:T(128)}) %tuple.28), condition=%wide.region_8.9_spmd.clone, body=%wide.region_7.8_spmd.clone.sunk | while | flops 2820276224 | bytes 12320821 | solution.py:128
  222.9 1.9 fusion.51
  228.4 1.9 fusion.51
  234.0 1.9 fusion.51
  239.5 1.9 fusion.51
  245.0 2.0 fusion.20
  247.1 35.5 %all-gather.3.cloned.1.call-done = bf16[32,256,128]{2,1,0:T(8,128)(2,1)} async-done(((bf16[4,256,128]{2,1,0:T(8,128)(2,1)}), bf16[32,256,128]{2,1,0:T(8,128)(2,1)}) %all-gather.3.cloned.1.call-update) | async-done | bytes 2097168 | tf_op jit(solution)/shard_map/all_gather | solution.py:135
  282.6 90.0 %all-gather.5.cloned.1.call-done = bf16[128,256,128]{2,1,0:T(8,128)(2,1)} async-done(((bf16[32,256,128]{2,1,0:T(8,128)(2,1)}), bf16[128,256,128]{2,1,0:T(8,128)(2,1)}) %all-gather.5.cloned.1.call-update) | async-done | bytes 8388624 | tf_op jit(solution)/shard_map/all_gather | solution.py:136
  372.5 6.5 %gather_fusion.1 = bf16[64,256,128]{2,1,0:T(8,128)(2,1)} fusion(bf16[128,256,128]{2,1,0:T(8,128)(2,1)} %all-gather.5.cloned.1.call-done, s32[1024]{0:T(1024)S(1)} %pad_clamp_fusion), kind=kCustom, calls=%fused_computation.1 | custom fusion | bytes 8388864 | tf_op jit(solution)/shard_map/jit(_take)/gather | solution.py:137
  (61 shorter events, 23.5 us)
Async XLA Ops:
  7.2 177.7 %reduce-scatter.2.cloned.1.call-start = ((), (), s32[]{:S(2)}) async-start(), calls=%async_computation.2 | async-start | bytes 4718592 | tf_op jit(solution)/shard_map/reduce_scatter | solution.py:119
  121.9 63.0 %copy-start = (f32[1,4,256,128]{3,2,1,0:T(8,128)S(1)}, f32[1,4,256,128]{3,2,1,0:T(8,128)}, u32[]{:S(2)}) copy-start(f32[1,4,256,128]{3,2,1,0:T(8,128)} %param.8) | copy-start | bytes 1572868
  125.5 157.0 %all-gather.3.cloned.1.call-start = ((), (), s32[]{:S(2)}) async-start(), calls=%async_computation.3 | async-start | bytes 2359296 | tf_op jit(solution)/shard_map/all_gather | solution.py:135
  184.8 35.8 %copy-start.1 = (f32[4,256,128]{2,1,0:T(8,128)S(1)}, f32[4,256,128]{2,1,0:T(8,128)}, u32[]{:S(2)}) copy-start(f32[4,256,128]{2,1,0:T(8,128)} %reduce-scatter.2.cloned.1.call-done) | copy-start | bytes 1572868
  187.3 2.3 collective-permute-start
  189.8 7.6 %collective-permute-start.1 = (f32[4,64,256]{2,1,0:T(8,128)S(1)}, f32[4,64,256]{2,1,0:T(8,128)S(1)}, u32[]{:S(2)}, u32[]{:S(2)}) collective-permute-start(f32[4,64,256]{2,1,0:T(8,128)S(1)} %slice_select_fusion.1), channel_id=1, source_target_pairs={{0,2},{1,3},{2,0},{3,1},{4,6},{5,7},{6,4},{7,5},{8,10},{9,11},{10,... | collective-permute-start | bytes 786440 | tf_op jit(solution)/shard_map/ppermute | solution.py:65
  197.4 5.4 %collective-permute-start.2 = (f32[4,32,256]{2,1,0:T(8,128)S(1)}, f32[4,32,256]{2,1,0:T(8,128)S(1)}, u32[]{:S(2)}, u32[]{:S(2)}) collective-permute-start(f32[4,32,256]{2,1,0:T(8,128)S(1)} %slice_select_fusion.2), channel_id=1, source_target_pairs={{0,4},{1,5},{2,6},{3,7},{4,0},{5,1},{6,2},{7,3},{8,12},{9,13},{10,... | collective-permute-start | bytes 393224 | tf_op jit(solution)/shard_map/ppermute | solution.py:65
  202.9 5.4 %collective-permute-start.3 = (f32[4,32,256]{2,1,0:T(8,128)S(1)}, f32[4,32,256]{2,1,0:T(8,128)S(1)}, u32[]{:S(2)}, u32[]{:S(2)}) collective-permute-start(f32[4,32,256]{2,1,0:T(8,128)S(1)} %select_add_fusion.2), channel_id=1, source_target_pairs={{0,4},{1,5},{2,6},{3,7},{4,0},{5,1},{6,2},{7,3},{8,12},{9,13},{10,... | collective-permute-start | bytes 393224 | tf_op jit(solution)/shard_map/ppermute | solution.py:69
  208.3 5.7 %collective-permute-start.4 = (f32[4,64,256]{2,1,0:T(8,128)S(1)}, f32[4,64,256]{2,1,0:T(8,128)S(1)}, u32[]{:S(2)}, u32[]{:S(2)}) collective-permute-start(f32[4,64,256]{2,1,0:T(8,128)S(1)} %maximum_select_fusion.2), channel_id=1, source_target_pairs={{0,2},{1,3},{2,0},{3,1},{4,6},{5,7},{6,4},{7,5},{8,10},{9,11},{10,... | collective-permute-start | bytes 786440 | tf_op jit(solution)/shard_map/ppermute | solution.py:69
  214.1 6.1 %collective-permute-start.5 = (f32[4,128,256]{2,1,0:T(8,128)S(1)}, f32[4,128,256]{2,1,0:T(8,128)S(1)}, u32[]{:S(2)}, u32[]{:S(2)}) collective-permute-start(f32[4,128,256]{2,1,0:T(8,128)S(1)} %maximum_select_fusion.1), channel_id=1, source_target_pairs={{0,1},{1,0},{2,3},{3,2},{4,5},{5,4},{6,7},{7,6},{8,9},{9,8},{10,11... | collective-permute-start | bytes 1572872 | tf_op jit(solution)/shard_map/ppermute | solution.py:69
  221.6 23.4 %copy-start.2 = (f32[1,4,256,128]{3,2,1,0:T(8,128)S(1)}, f32[1,4,256,128]{3,2,1,0:T(8,128)}, u32[]{:S(2)}) copy-start(f32[1,4,256,128]{3,2,1,0:T(8,128)} %param.9) | copy-start | bytes 1572868
  243.7 38.8 %copy-start.3 = (s32[64,1]{0,1:T(1,128)S(1)}, s32[64,1]{0,1:T(1,128)}, u32[]{:S(2)}) copy-start(s32[64,1]{0,1:T(1,128)} %param.7) | copy-start | bytes 772
  247.0 125.5 %all-gather.5.cloned.1.call-start = ((), (), s32[]{:S(2)}) async-start(), calls=%async_computation.4 | async-start | bytes 10485760 | tf_op jit(solution)/shard_map/all_gather | solution.py:136
Sparse Core Ops, SparseCore 0:
  125.6 59.1 reduce-scatter.1
  247.1 35.3 all-gather.2
  284.3 88.1 all-gather.4

commit v6 on v2

--- a/solution.py
+++ b/solution.py
@@ -47,8 +47,38 @@
     )
 
 
+def own_sum(total):
+    size = lax.axis_size("own")
+    index = lax.axis_index("own")
+    rows = total.shape[1]
+    core_pairs = [(i, i ^ 1) for i in range(size)]
+    high = (index & 1) != 0
+    lower, upper = total[:, : rows // 2], total[:, rows // 2 :]
+    keep = jnp.where(high, upper, lower)
+    total = keep + lax.ppermute(jnp.where(high, lower, upper), "own", core_pairs)
+    chips = size // 2
+    chip = index // 2
+    piece = total.shape[1] // chips
+    quarters = total.reshape(total.shape[0], chips, piece, total.shape[2])
+    summed = jnp.take(quarters, chip, axis=1, mode="clip")
+    for shift in range(1, chips):
+        pairs = [(i, i ^ (2 * shift)) for i in range(size)]
+        summed = summed + lax.ppermute(
+            jnp.take(quarters, chip ^ shift, axis=1, mode="clip"), "own", pairs
+        )
+    arrived = [summed]
+    for shift in range(1, chips):
+        pairs = [(i, i ^ (2 * shift)) for i in range(size)]
+        arrived.append(lax.ppermute(summed, "own", pairs))
+    arrived = jnp.stack(arrived, axis=1)
+    order = jnp.arange(chips, dtype=jnp.int32) ^ chip
+    total = jnp.take(arrived, order, axis=1, mode="clip").reshape(total.shape)
+    other = lax.ppermute(total, "own", core_pairs)
+    return jnp.where(high, jnp.concatenate([other, total], axis=1), jnp.concatenate([total, other], axis=1))
+
+
 def gram_total(values):
-    return lax.psum(local_gram(values), "own")
+    return own_sum(local_gram(values))
 
 
 def matmul(left, right):
@@ -87,7 +117,7 @@
     owner_list = owner[:, 0]
     target = slot_targets(owner_list, group_count, slot_count)
     present, source = slot_sources(target, group_count * slot_count, block_count)
-    outgoing = jnp.where(present[:, None, None], jnp.take(local_rows, source, axis=0), 0)
+    outgoing = jnp.where(present[:, None, None], jnp.take(local_rows, source, axis=0, mode="clip"), 0)
     row_count = lax.axis_size("x")
     outgoing = outgoing.reshape((row_count, -1) + outgoing.shape[1:])
     arrived = lax.all_to_all(outgoing, "x", 0, 0, tiled=True)
@@ -101,13 +131,15 @@
     ortho = update * factor[:, None, None]
     gram = update_gram * (factor * factor)[:, None, None]
     eye = jnp.eye(block_rows, dtype=jnp.float32)[None]
-    for iteration in range(ITERS):
-        ortho, gram = newton_turn(ortho, gram, eye, iteration < ITERS - 1)
+    ortho, gram = lax.fori_loop(
+        0, ITERS - 1, lambda _, carry: newton_turn(*carry, eye, True), (ortho, gram)
+    )
+    ortho, gram = newton_turn(ortho, gram, eye, False)
     step_factor = STEP_SIZE * 0.2 * math.sqrt(max(block_rows, D))
     master_new = master[0] * (1.0 - STEP_SIZE * DECAY) - step_factor * ortho
     weights_low = master_new.astype(jnp.bfloat16)
     every_slot = lax.all_gather(weights_low, ("x", "z"), axis=0, tiled=True)
-    weights = jnp.take(every_slot, target, axis=0)
+    weights = jnp.take(every_slot, target, axis=0, mode="clip")
     return (momentum_new[None], master_new[None], weights)
 
 

time: 394 us -> 348 us (0.88)
  waiting for transfers between devices: 220 us -> 168 us
  starting transfers between devices: 0.3 us -> 11.3 us
    psum x1 -> x0, waiting for transfers between devices: 64.4 us -> none  [gram_total(): return lax.psum(local_gram(values), 'own')]
    ppermute x0 -> x8, waiting for transfers between devices: none -> 13.4 us  [the longest x3 5.84 us: own_sum(): lax.ppermute(jnp.take(quarters, chip ^ shift, axis=1, mode='clip'), 'own'...]
    ppermute x0 -> x8, starting transfers between devices: none -> 11.2 us  [the longest x1 3.71 us: own_sum(): other = lax.ppermute(total, 'own', core_pairs)]
    select_n x3 -> x2, other arithmetic: 9.31 us -> 7.31 us  [the longest x1 7.24 us: on_device(): jnp.where(present[:, None, None], jnp.take(local_rows, source, axis=0, mo...]
    gather x2 -> x5, local copies, waits for them, and re-layouts: 15.1 us -> 15.8 us  [the longest x1 8.63 us: on_device(): jnp.take(local_rows, source, axis=0, mode='clip')]
  transfers between devices with their start and end apart: 3 -> 10, of which waited for: 3 -> 9; matrix products, arithmetic and copies ran while one was open for 0% -> 0% of each run, Pallas kernels for 0% -> 0%
where the time goes in v6:
time: 348 us
  waiting for transfers between devices  168 us (48%)
  blocking collectives  96.2 us (28%)
  matrix products  27.3 us (8%)
  local copies, waits for them, and re-layouts  16 us (5%)
  other arithmetic  15.1 us (4%)
  between operations  14.2 us (4%)
  starting transfers between devices  11.3 us (3%)
    all_to_all x1, blocking collectives, on_device(): arrived = lax.all_to_all(outgoing, 'x', 0, 0, tiled=True)  96.2 us
    all_gather x1, waiting for transfers between devices, on_device(): every_slot = lax.all_gather(weights_low, ('x', 'z'), axis=0, tiled=True)  94.8 us
    reduce_scatter x1, waiting for transfers between devices, on_device(): gradient = lax.psum_scatter(row_sum, 'z', scatter_dimension=0, tiled=True)  59.3 us
    dot_general x13, matrix products, matmul(): jnp.einsum('srt,stu->sru', left, right, precision=lax.Precision.HIGHEST,...  18.7 us
    gather x1, local copies, waits for them, and re-layouts, on_device(): jnp.take(local_rows, source, axis=0, mode='clip')  8.63 us
    select_n x1, other arithmetic, on_device(): jnp.where(present[:, None, None], jnp.take(local_rows, source, axis=0, mo...  7.24 us
  transfers between devices with their start and end apart: 10, of which 9 were waited for; matrix products, arithmetic and copies ran while one was open for 0% of the time, Pallas kernels for 0%

profile of v6, /device:TPU:1, one launch (start us, length us, event | category | flops | bytes accessed | tf_op | source)
XLA Modules:
  0.0 347.9 jit_solution(4420394047383528219)
XLA Ops:
  9.8 8.6 %gather_fusion = bf16[128,256,128]{2,1,0:T(8,128)(2,1)} fusion(bf16[64,256,128]{2,1,0:T(8,128)(2,1)} %bitcast.78, s32[1024]{0:T(1024)S(1)} %pad_clamp_fusion.2), kind=kCustom, calls=%fused_computation | custom fusion | bytes 16777728 | tf_op jit(solution)/shard_map/jit(_take)/gather | solution.py:120
  18.5 7.2 %broadcast_select_fusion = bf16[4,32,256,128]{3,2,1,0:T(8,128)(2,1)} fusion(bf16[4,32,256,128]{3,2,1,0:T(8,128)(2,1)} %bitcast.77, pred[4,32]{1,0:T(4,128)(4,1)S(1)} %broadcast_in_dim.70), kind=kLoop, calls=%fused_computation.16 | loop fusion | flops 4194304 | bytes 16777344 | tf_op jit(solution)/shard_map/jit(_where)/select_n | solution.py:120
  25.7 96.2 %all_to_all.5 = bf16[4,32,256,128]{3,2,1,0:T(8,128)(2,1)S(1)} all-to-all(bf16[4,32,256,128]{3,2,1,0:T(8,128)(2,1)} %broadcast_select_fusion), channel_id=1, replica_groups=mesh['x'=4,'z'=8,'own'=8] {'x'}, dimensions={0} | all-to-all | bytes 16777216 | tf_op jit(solution)/shard_map/all_to_all | solution.py:123
  121.9 3.6 %convert_reduce_fusion = f32[32,256,128]{2,1,0:T(8,128)} fusion(bf16[4,32,256,128]{3,2,1,0:T(8,128)(2,1)S(1)} %all_to_all.5), kind=kLoop, calls=%fused_computation.15 | loop fusion | flops 7340032 | bytes 12582912 | tf_op jit(solution)/shard_map/reduce_sum | solution.py:124
  125.6 59.3 %reduce-scatter.2.cloned.1.call-done = f32[4,256,128]{2,1,0:T(8,128)} async-done(((f32[32,256,128]{2,1,0:T(8,128)}), f32[4,256,128]{2,1,0:T(8,128)}) %reduce-scatter.2.cloned.1.call-update) | async-done | bytes 524304 | tf_op jit(solution)/shard_map/reduce_scatter | solution.py:125
  184.8 2.4 fusion.14
  188.1 1.5 collective-permute-done
  189.8 2.6 collective-permute-start.3
  193.1 4.6 %collective-permute-done.3 = f32[4,32,256]{2,1,0:T(8,128)S(1)} collective-permute-done((f32[4,32,256]{2,1,0:T(8,128)S(1)}, f32[4,32,256]{2,1,0:T(8,128)S(1)}, u32[]{:S(2)}, u32[]{:S(2)}) %collective-permute-start.3) | collective-permute-done | bytes 131104 | tf_op jit(solution)/shard_map/ppermute | solution.py:66
  199.0 2.5 collective-permute-start.6
  202.3 3.1 collective-permute-done.6
  205.4 1.5 collective-permute-done.5
  207.6 3.7 %collective-permute-start.7 = (f32[4,128,256]{2,1,0:T(8,128)S(1)}, f32[4,128,256]{2,1,0:T(8,128)S(1)}, u32[]{:S(2)}, u32[]{:S(2)}) collective-permute-start(f32[4,128,256]{2,1,0:T(8,128)S(1)} %bitcast.79), channel_id=1, source_target_pairs={{0,1},{1,0},{2,3},{3,2},{4,5},{5,4},{6,7},{7,6},{8,9},{9,8},{10,11... | collective-permute-start | bytes 1572872 | tf_op jit(solution)/shard_map/ppermute | solution.py:76
  211.3 1.5 collective-permute-done.7
  214.3 22.2 %while.17 = (s32[]{:T(128)}, f32[4,256,128]{2,1,0:T(8,128)S(1)}, f32[4,256,256]{2,1,0:T(8,128)S(1)}, s32[]{:T(128)}) while((s32[]{:T(128)}, f32[4,256,128]{2,1,0:T(8,128)S(1)}, f32[4,256,256]{2,1,0:T(8,128)S(1)}, s32[]{:T(128)}) %tuple.50), condition=%wide.region_8.9_spmd.clone, body=%wide.region_7.8_spmd.clone.sunk | while | flops 2820276224 | bytes 12320821 | solution.py:134
  216.7 1.9 fusion.53
  219.8 1.3 fusion.52
  222.2 1.9 fusion.53
  227.8 1.9 fusion.53
  233.3 1.9 fusion.53
  236.4 1.3 fusion.9
  237.7 2.0 fusion.22
  239.7 94.8 %all-gather.2.cloned.1.call-done = bf16[128,256,128]{2,1,0:T(8,128)(2,1)} async-done(((bf16[4,256,128]{2,1,0:T(8,128)(2,1)}), bf16[128,256,128]{2,1,0:T(8,128)(2,1)}) %all-gather.2.cloned.1.call-update) | async-done | bytes 8388624 | tf_op jit(solution)/shard_map/all_gather | solution.py:141
  334.5 6.5 %gather_fusion.2 = bf16[64,256,128]{2,1,0:T(8,128)(2,1)} fusion(bf16[128,256,128]{2,1,0:T(8,128)(2,1)} %all-gather.2.cloned.1.call-done, s32[1024]{0:T(1024)S(1)} %pad_clamp_fusion), kind=kCustom, calls=%fused_computation.2 | custom fusion | bytes 8388864 | tf_op jit(solution)/shard_map/jit(_take)/gather | solution.py:142
  (63 shorter events, 21.8 us)
Async XLA Ops:
  7.2 177.7 %reduce-scatter.2.cloned.1.call-start = ((), (), s32[]{:S(2)}) async-start(), calls=%async_computation.2 | async-start | bytes 4718592 | tf_op jit(solution)/shard_map/reduce_scatter | solution.py:125
  121.9 63.0 %copy-start = (f32[1,4,256,128]{3,2,1,0:T(8,128)S(1)}, f32[1,4,256,128]{3,2,1,0:T(8,128)}, u32[]{:S(2)}) copy-start(f32[1,4,256,128]{3,2,1,0:T(8,128)} %param.8) | copy-start | bytes 1572868
  125.5 209.1 %all-gather.2.cloned.1.call-start = ((), (), s32[]{:S(2)}) async-start(), calls=%async_computation.3 | async-start | bytes 8650752 | tf_op jit(solution)/shard_map/all_gather | solution.py:141
  184.8 28.3 %copy-start.1 = (f32[4,256,128]{2,1,0:T(8,128)S(1)}, f32[4,256,128]{2,1,0:T(8,128)}, u32[]{:S(2)}) copy-start(f32[4,256,128]{2,1,0:T(8,128)} %reduce-scatter.2.cloned.1.call-done) | copy-start | bytes 1572868
  187.3 2.3 collective-permute-start
  189.8 8.0 %collective-permute-start.3 = (f32[4,32,256]{2,1,0:T(8,128)S(1)}, f32[4,32,256]{2,1,0:T(8,128)S(1)}, u32[]{:S(2)}, u32[]{:S(2)}) collective-permute-start(f32[4,32,256]{2,1,0:T(8,128)S(1)} %get-tuple-element.91), channel_id=1, source_target_pairs={{0,6},{1,7},{2,4},{3,5},{4,2},{5,3},{6,0},{7,1},{8,14},{9,15},{10,... | collective-permute-start | bytes 393224 | tf_op jit(solution)/shard_map/ppermute | solution.py:66
  192.3 5.9 %collective-permute-start.2 = (f32[4,32,256]{2,1,0:T(8,128)S(1)}, f32[4,32,256]{2,1,0:T(8,128)S(1)}, u32[]{:S(2)}, u32[]{:S(2)}) collective-permute-start(f32[4,32,256]{2,1,0:T(8,128)S(1)} %get-tuple-element.92), channel_id=1, source_target_pairs={{0,4},{1,5},{2,6},{3,7},{4,0},{5,1},{6,2},{7,3},{8,12},{9,13},{10,... | collective-permute-start | bytes 393224 | tf_op jit(solution)/shard_map/ppermute | solution.py:66
  192.9 6.1 %collective-permute-start.1 = (f32[4,32,256]{2,1,0:T(8,128)S(1)}, f32[4,32,256]{2,1,0:T(8,128)S(1)}, u32[]{:S(2)}, u32[]{:S(2)}) collective-permute-start(f32[4,32,256]{2,1,0:T(8,128)S(1)} %get-tuple-element.90), channel_id=1, source_target_pairs={{0,2},{1,3},{2,0},{3,1},{4,6},{5,7},{6,4},{7,5},{8,10},{9,11},{10,... | collective-permute-start | bytes 393224 | tf_op jit(solution)/shard_map/ppermute | solution.py:66
  199.0 6.4 %collective-permute-start.6 = (f32[4,32,256]{2,1,0:T(8,128)S(1)}, f32[4,32,256]{2,1,0:T(8,128)S(1)}, u32[]{:S(2)}, u32[]{:S(2)}) collective-permute-start(f32[4,32,256]{2,1,0:T(8,128)S(1)} %fusion.16), channel_id=1, source_target_pairs={{0,6},{1,7},{2,4},{3,5},{4,2},{5,3},{6,0},{7,1},{8,14},{9,15},{10,... | collective-permute-start | bytes 393224 | tf_op jit(solution)/shard_map/ppermute | solution.py:72
  201.5 5.4 %collective-permute-start.5 = (f32[4,32,256]{2,1,0:T(8,128)S(1)}, f32[4,32,256]{2,1,0:T(8,128)S(1)}, u32[]{:S(2)}, u32[]{:S(2)}) collective-permute-start(f32[4,32,256]{2,1,0:T(8,128)S(1)} %fusion.16), channel_id=1, source_target_pairs={{0,4},{1,5},{2,6},{3,7},{4,0},{5,1},{6,2},{7,3},{8,12},{9,13},{10,... | collective-permute-start | bytes 393224 | tf_op jit(solution)/shard_map/ppermute | solution.py:72
  202.1 4.8 %collective-permute-start.4 = (f32[4,32,256]{2,1,0:T(8,128)S(1)}, f32[4,32,256]{2,1,0:T(8,128)S(1)}, u32[]{:S(2)}, u32[]{:S(2)}) collective-permute-start(f32[4,32,256]{2,1,0:T(8,128)S(1)} %fusion.16), channel_id=1, source_target_pairs={{0,2},{1,3},{2,0},{3,1},{4,6},{5,7},{6,4},{7,5},{8,10},{9,11},{10,... | collective-permute-start | bytes 393224 | tf_op jit(solution)/shard_map/ppermute | solution.py:72
  207.6 5.2 %collective-permute-start.7 = (f32[4,128,256]{2,1,0:T(8,128)S(1)}, f32[4,128,256]{2,1,0:T(8,128)S(1)}, u32[]{:S(2)}, u32[]{:S(2)}) collective-permute-start(f32[4,128,256]{2,1,0:T(8,128)S(1)} %bitcast.79), channel_id=1, source_target_pairs={{0,1},{1,0},{2,3},{3,2},{4,5},{5,4},{6,7},{7,6},{8,9},{9,8},{10,11... | collective-permute-start | bytes 1572872 | tf_op jit(solution)/shard_map/ppermute | solution.py:76
  214.2 23.5 %copy-start.2 = (f32[1,4,256,128]{3,2,1,0:T(8,128)S(1)}, f32[1,4,256,128]{3,2,1,0:T(8,128)}, u32[]{:S(2)}) copy-start(f32[1,4,256,128]{3,2,1,0:T(8,128)} %param.9) | copy-start | bytes 1572868
  214.3 25.4 %copy-start.3 = (s32[64,1]{0,1:T(1,128)S(1)}, s32[64,1]{0,1:T(1,128)}, u32[]{:S(2)}) copy-start(s32[64,1]{0,1:T(1,128)} %param.7) | copy-start | bytes 772
Sparse Core Ops, SparseCore 0:
  125.6 59.1 reduce-scatter.1
  239.8 94.6 all-gather.1

commit v7 on v6

--- a/solution.py
+++ b/solution.py
@@ -117,11 +117,12 @@
     owner_list = owner[:, 0]
     target = slot_targets(owner_list, group_count, slot_count)
     present, source = slot_sources(target, group_count * slot_count, block_count)
-    outgoing = jnp.where(present[:, None, None], jnp.take(local_rows, source, axis=0, mode="clip"), 0)
+    outgoing = jnp.take(local_rows, source, axis=0, mode="clip")
     row_count = lax.axis_size("x")
     outgoing = outgoing.reshape((row_count, -1) + outgoing.shape[1:])
     arrived = lax.all_to_all(outgoing, "x", 0, 0, tiled=True)
-    row_sum = jnp.sum(arrived.astype(jnp.float32), axis=0)
+    row_present = jnp.take(present.reshape(row_count, -1), lax.axis_index("x"), axis=0, mode="clip")
+    row_sum = jnp.where(row_present[:, None, None], jnp.sum(arrived.astype(jnp.float32), axis=0), 0.0)
     gradient = lax.psum_scatter(row_sum, "z", scatter_dimension=0, tiled=True)
     momentum_new = BETA * momentum[0] + gradient
     update = gradient + BETA * momentum_new

time: 348 us -> 346 us (level)
  blocking collectives: 96.2 us -> 0 us
  waiting for transfers between devices: 168 us -> 259 us
  starting transfers between devices: 11.3 us -> 16.9 us
    all_to_all x1 -> x0, blocking collectives: 96.2 us -> none  [on_device(): arrived = lax.all_to_all(outgoing, 'x', 0, 0, tiled=True)]
    all_to_all x0 -> x1, waiting for transfers between devices: none -> 91.6 us  [on_device(): arrived = lax.all_to_all(outgoing, 'x', 0, 0, tiled=True)]
    all_to_all x0 -> x1, starting transfers between devices: none -> 5.63 us  [on_device(): arrived = lax.all_to_all(outgoing, 'x', 0, 0, tiled=True)]
    select_n x1, other arithmetic: 7.24 us -> 2.48 us  [on_device(): jnp.where(row_present[:, None, None], jnp.sum(arrived.astype(jnp.float32)...]
    gather x1 -> x2, local copies, waits for them, and re-layouts: 8.63 us -> 8.63 us  [the longest x1 8.62 us: on_device(): outgoing = jnp.take(local_rows, source, axis=0, mode='clip')]
  transfers between devices with their start and end apart: 10 -> 11, of which waited for: 9 -> 10; matrix products, arithmetic and copies ran while one was open for 0% -> 0% of each run, Pallas kernels for 0% -> 0%
where the time goes in v7:
time: 346 us
  waiting for transfers between devices  259 us (75%)
  matrix products  27.2 us (8%)
  starting transfers between devices  16.9 us (5%)
  local copies, waits for them, and re-layouts  16 us (5%)
  between operations  14.2 us (4%)
  other arithmetic  12.2 us (4%)
    all_gather x1, waiting for transfers between devices, on_device(): every_slot = lax.all_gather(weights_low, ('x', 'z'), axis=0, tiled=True)  94.8 us
    all_to_all x1, waiting for transfers between devices, on_device(): arrived = lax.all_to_all(outgoing, 'x', 0, 0, tiled=True)  91.6 us
    reduce_scatter x1, waiting for transfers between devices, on_device(): gradient = lax.psum_scatter(row_sum, 'z', scatter_dimension=0, tiled=True)  59.5 us
    dot_general x13, matrix products, matmul(): jnp.einsum('srt,stu->sru', left, right, precision=lax.Precision.HIGHEST,...  18.7 us
    gather x1, local copies, waits for them, and re-layouts, on_device(): outgoing = jnp.take(local_rows, source, axis=0, mode='clip')  8.62 us
  transfers between devices with their start and end apart: 11, of which 10 were waited for; matrix products, arithmetic and copies ran while one was open for 0% of the time, Pallas kernels for 0%

profile of v7, /device:TPU:1, one launch (start us, length us, event | category | flops | bytes accessed | tf_op | source)
XLA Modules:
  0.0 346.2 jit_solution(5090245271245332423)
XLA Ops:
  9.6 8.6 %gather_fusion = bf16[128,256,128]{2,1,0:T(8,128)(2,1)} fusion(bf16[64,256,128]{2,1,0:T(8,128)(2,1)} %bitcast.80, s32[1024]{0:T(1024)S(1)} %pad_clamp_fusion.2), kind=kCustom, calls=%fused_computation | custom fusion | bytes 16777728 | tf_op jit(solution)/shard_map/jit(_take)/gather | solution.py:120
  18.2 5.6 %all-to-all-start = ((bf16[4,32,256,128]{3,2,1,0:T(8,128)(2,1)}), bf16[4,32,256,128]{3,2,1,0:T(8,128)(2,1)}, u32[]{:S(2)}, u32[]{:S(2)}) async-start(bf16[4,32,256,128]{3,2,1,0:T(8,128)(2,1)} %bitcast.79), calls=%async_computation | async-start | bytes 16777216 | tf_op jit(solution)/shard_map/all_to_all | solution.py:123
  24.1 91.6 %all-to-all-done = bf16[4,32,256,128]{3,2,1,0:T(8,128)(2,1)} async-done(((bf16[4,32,256,128]{3,2,1,0:T(8,128)(2,1)}), bf16[4,32,256,128]{3,2,1,0:T(8,128)(2,1)}, u32[]{:S(2)}, u32[]{:S(2)}) %all-to-all-start) | async-done | bytes 8388640 | tf_op jit(solution)/shard_map/all_to_all | solution.py:123
  115.8 5.4 %convert_reduce_fusion = f32[32,256,128]{2,1,0:T(8,128)S(1)} fusion(bf16[4,32,256,128]{3,2,1,0:T(8,128)(2,1)} %all-to-all-done), kind=kLoop, calls=%fused_computation.15 | loop fusion | flops 7340032 | bytes 12582912 | tf_op jit(solution)/shard_map/reduce_sum | solution.py:125
  121.1 2.5 broadcast_select_fusion
  123.7 59.5 %reduce-scatter.2.cloned.1.call-done = f32[4,256,128]{2,1,0:T(8,128)} async-done(((f32[32,256,128]{2,1,0:T(8,128)}), f32[4,256,128]{2,1,0:T(8,128)}) %reduce-scatter.2.cloned.1.call-update) | async-done | bytes 524304 | tf_op jit(solution)/shard_map/reduce_scatter | solution.py:126
  183.2 2.3 fusion.14
  186.4 1.5 collective-permute-done
  188.1 2.6 collective-permute-start.3
  191.4 4.6 %collective-permute-done.3 = f32[4,32,256]{2,1,0:T(8,128)S(1)} collective-permute-done((f32[4,32,256]{2,1,0:T(8,128)S(1)}, f32[4,32,256]{2,1,0:T(8,128)S(1)}, u32[]{:S(2)}, u32[]{:S(2)}) %collective-permute-start.3) | collective-permute-done | bytes 131104 | tf_op jit(solution)/shard_map/ppermute | solution.py:66
  197.3 2.5 collective-permute-start.6
  200.7 3.1 collective-permute-done.6
  203.7 1.5 collective-permute-done.5
  205.9 3.7 %collective-permute-start.7 = (f32[4,128,256]{2,1,0:T(8,128)S(1)}, f32[4,128,256]{2,1,0:T(8,128)S(1)}, u32[]{:S(2)}, u32[]{:S(2)}) collective-permute-start(f32[4,128,256]{2,1,0:T(8,128)S(1)} %bitcast.81), channel_id=1, source_target_pairs={{0,1},{1,0},{2,3},{3,2},{4,5},{5,4},{6,7},{7,6},{8,9},{9,8},{10,11... | collective-permute-start | bytes 1572872 | tf_op jit(solution)/shard_map/ppermute | solution.py:76
  209.6 1.5 collective-permute-done.7
  212.6 22.2 %while.18 = (s32[]{:T(128)}, f32[4,256,128]{2,1,0:T(8,128)S(1)}, f32[4,256,256]{2,1,0:T(8,128)S(1)}, s32[]{:T(128)}) while((s32[]{:T(128)}, f32[4,256,128]{2,1,0:T(8,128)S(1)}, f32[4,256,256]{2,1,0:T(8,128)S(1)}, s32[]{:T(128)}) %tuple.55), condition=%wide.region_8.9_spmd.clone, body=%wide.region_7.8_spmd.clone.sunk | while | flops 2820276224 | bytes 12320821 | solution.py:135
  215.0 1.9 fusion.53
  218.1 1.3 fusion.52
  220.5 1.9 fusion.53
  226.1 1.9 fusion.53
  231.6 1.9 fusion.53
  236.0 2.0 fusion.22
  238.0 94.8 %all-gather.2.cloned.1.call-done = bf16[128,256,128]{2,1,0:T(8,128)(2,1)} async-done(((bf16[4,256,128]{2,1,0:T(8,128)(2,1)}), bf16[128,256,128]{2,1,0:T(8,128)(2,1)}) %all-gather.2.cloned.1.call-update) | async-done | bytes 8388624 | tf_op jit(solution)/shard_map/all_gather | solution.py:142
  332.8 6.5 %gather_fusion.2 = bf16[64,256,128]{2,1,0:T(8,128)(2,1)} fusion(bf16[128,256,128]{2,1,0:T(8,128)(2,1)} %all-gather.2.cloned.1.call-done, s32[1024]{0:T(1024)S(1)} %pad_clamp_fusion), kind=kCustom, calls=%fused_computation.2 | custom fusion | bytes 8388864 | tf_op jit(solution)/shard_map/jit(_take)/gather | solution.py:143
  (65 shorter events, 23.1 us)
Async XLA Ops:
  18.2 97.5 %all-to-all-start = ((bf16[4,32,256,128]{3,2,1,0:T(8,128)(2,1)}), bf16[4,32,256,128]{3,2,1,0:T(8,128)(2,1)}, u32[]{:S(2)}, u32[]{:S(2)}) async-start(bf16[4,32,256,128]{3,2,1,0:T(8,128)(2,1)} %bitcast.79), calls=%async_computation | async-start | bytes 16777216 | tf_op jit(solution)/shard_map/all_to_all | solution.py:123
  23.9 159.3 %reduce-scatter.2.cloned.1.call-start = ((), (), s32[]{:S(2)}) async-start(), calls=%async_computation.2 | async-start | bytes 4718592 | tf_op jit(solution)/shard_map/reduce_scatter | solution.py:126
  123.6 59.6 %copy-start = (f32[1,4,256,128]{3,2,1,0:T(8,128)S(1)}, f32[1,4,256,128]{3,2,1,0:T(8,128)}, u32[]{:S(2)}) copy-start(f32[1,4,256,128]{3,2,1,0:T(8,128)} %param.8) | copy-start | bytes 1572868
  123.6 209.2 %all-gather.2.cloned.1.call-start = ((), (), s32[]{:S(2)}) async-start(), calls=%async_computation.3 | async-start | bytes 8650752 | tf_op jit(solution)/shard_map/all_gather | solution.py:142
  185.6 25.9 %copy-start.1 = (f32[4,256,128]{2,1,0:T(8,128)S(1)}, f32[4,256,128]{2,1,0:T(8,128)}, u32[]{:S(2)}) copy-start(f32[4,256,128]{2,1,0:T(8,128)} %reduce-scatter.2.cloned.1.call-done) | copy-start | bytes 1572868
  185.6 2.3 collective-permute-start
  188.1 8.0 %collective-permute-start.3 = (f32[4,32,256]{2,1,0:T(8,128)S(1)}, f32[4,32,256]{2,1,0:T(8,128)S(1)}, u32[]{:S(2)}, u32[]{:S(2)}) collective-permute-start(f32[4,32,256]{2,1,0:T(8,128)S(1)} %get-tuple-element.102), channel_id=1, source_target_pairs={{0,6},{1,7},{2,4},{3,5},{4,2},{5,3},{6,0},{7,1},{8,14},{9,15},{10,... | collective-permute-start | bytes 393224 | tf_op jit(solution)/shard_map/ppermute | solution.py:66
  190.6 5.9 %collective-permute-start.2 = (f32[4,32,256]{2,1,0:T(8,128)S(1)}, f32[4,32,256]{2,1,0:T(8,128)S(1)}, u32[]{:S(2)}, u32[]{:S(2)}) collective-permute-start(f32[4,32,256]{2,1,0:T(8,128)S(1)} %get-tuple-element.103), channel_id=1, source_target_pairs={{0,4},{1,5},{2,6},{3,7},{4,0},{5,1},{6,2},{7,3},{8,12},{9,13},{10,... | collective-permute-start | bytes 393224 | tf_op jit(solution)/shard_map/ppermute | solution.py:66
  191.2 6.1 %collective-permute-start.1 = (f32[4,32,256]{2,1,0:T(8,128)S(1)}, f32[4,32,256]{2,1,0:T(8,128)S(1)}, u32[]{:S(2)}, u32[]{:S(2)}) collective-permute-start(f32[4,32,256]{2,1,0:T(8,128)S(1)} %get-tuple-element.101), channel_id=1, source_target_pairs={{0,2},{1,3},{2,0},{3,1},{4,6},{5,7},{6,4},{7,5},{8,10},{9,11},{10,... | collective-permute-start | bytes 393224 | tf_op jit(solution)/shard_map/ppermute | solution.py:66
  197.3 6.4 %collective-permute-start.6 = (f32[4,32,256]{2,1,0:T(8,128)S(1)}, f32[4,32,256]{2,1,0:T(8,128)S(1)}, u32[]{:S(2)}, u32[]{:S(2)}) collective-permute-start(f32[4,32,256]{2,1,0:T(8,128)S(1)} %fusion.16), channel_id=1, source_target_pairs={{0,6},{1,7},{2,4},{3,5},{4,2},{5,3},{6,0},{7,1},{8,14},{9,15},{10,... | collective-permute-start | bytes 393224 | tf_op jit(solution)/shard_map/ppermute | solution.py:72
  199.8 5.4 %collective-permute-start.5 = (f32[4,32,256]{2,1,0:T(8,128)S(1)}, f32[4,32,256]{2,1,0:T(8,128)S(1)}, u32[]{:S(2)}, u32[]{:S(2)}) collective-permute-start(f32[4,32,256]{2,1,0:T(8,128)S(1)} %fusion.16), channel_id=1, source_target_pairs={{0,4},{1,5},{2,6},{3,7},{4,0},{5,1},{6,2},{7,3},{8,12},{9,13},{10,... | collective-permute-start | bytes 393224 | tf_op jit(solution)/shard_map/ppermute | solution.py:72
  200.4 4.8 %collective-permute-start.4 = (f32[4,32,256]{2,1,0:T(8,128)S(1)}, f32[4,32,256]{2,1,0:T(8,128)S(1)}, u32[]{:S(2)}, u32[]{:S(2)}) collective-permute-start(f32[4,32,256]{2,1,0:T(8,128)S(1)} %fusion.16), channel_id=1, source_target_pairs={{0,2},{1,3},{2,0},{3,1},{4,6},{5,7},{6,4},{7,5},{8,10},{9,11},{10,... | collective-permute-start | bytes 393224 | tf_op jit(solution)/shard_map/ppermute | solution.py:72
  205.9 5.2 %collective-permute-start.7 = (f32[4,128,256]{2,1,0:T(8,128)S(1)}, f32[4,128,256]{2,1,0:T(8,128)S(1)}, u32[]{:S(2)}, u32[]{:S(2)}) collective-permute-start(f32[4,128,256]{2,1,0:T(8,128)S(1)} %bitcast.81), channel_id=1, source_target_pairs={{0,1},{1,0},{2,3},{3,2},{4,5},{5,4},{6,7},{7,6},{8,9},{9,8},{10,11... | collective-permute-start | bytes 1572872 | tf_op jit(solution)/shard_map/ppermute | solution.py:76
  212.6 23.5 %copy-start.2 = (f32[1,4,256,128]{3,2,1,0:T(8,128)S(1)}, f32[1,4,256,128]{3,2,1,0:T(8,128)}, u32[]{:S(2)}) copy-start(f32[1,4,256,128]{3,2,1,0:T(8,128)} %param.9) | copy-start | bytes 1572868
  234.7 3.3 copy-start.3
Sparse Core Ops, SparseCore 0:
  123.8 59.3 reduce-scatter.1
  238.1 94.6 all-gather.1

commit v8 on v6

--- a/solution.py
+++ b/solution.py
@@ -117,11 +117,37 @@
     owner_list = owner[:, 0]
     target = slot_targets(owner_list, group_count, slot_count)
     present, source = slot_sources(target, group_count * slot_count, block_count)
-    outgoing = jnp.where(present[:, None, None], jnp.take(local_rows, source, axis=0, mode="clip"), 0)
     row_count = lax.axis_size("x")
-    outgoing = outgoing.reshape((row_count, -1) + outgoing.shape[1:])
-    arrived = lax.all_to_all(outgoing, "x", 0, 0, tiled=True)
-    row_sum = jnp.sum(arrived.astype(jnp.float32), axis=0)
+    row_slots = group_count * slot_count // row_count
+    width = row_slots * 3 // 4
+    row_of = target // row_slots
+    row_hot = (row_of[:, None] == jnp.arange(row_count, dtype=jnp.int32)[None, :]).astype(jnp.int32)
+    row_rank = jnp.sum((jnp.cumsum(row_hot, axis=0) - row_hot) * row_hot, axis=1)
+    fits = jnp.max(jnp.sum(row_hot, axis=0)) <= width
+    here = lax.axis_index("x")
+    row_present = jnp.take(present.reshape(row_count, -1), here, axis=0, mode="clip")
+
+    def padded(rows):
+        outgoing = jnp.take(rows, source, axis=0, mode="clip")
+        outgoing = outgoing.reshape((row_count, -1) + outgoing.shape[1:])
+        arrived = lax.all_to_all(outgoing, "x", 0, 0, tiled=True)
+        return jnp.where(row_present[:, None, None], jnp.sum(arrived.astype(jnp.float32), axis=0), 0.0)
+
+    def packed(rows):
+        spot = row_of * width + row_rank
+        hits = jnp.arange(row_count * width, dtype=jnp.int32)[:, None] == spot[None, :]
+        send_index = jnp.sum(jnp.where(hits, jnp.arange(block_count, dtype=jnp.int32)[None, :], 0), axis=1)
+        outgoing = jnp.take(rows, send_index, axis=0, mode="clip")
+        outgoing = outgoing.reshape((row_count, width) + outgoing.shape[1:])
+        arrived = lax.all_to_all(outgoing, "x", 0, 0, tiled=True)
+        packed_sum = jnp.sum(arrived.astype(jnp.float32), axis=0)
+        slots_here = here * row_slots + jnp.arange(row_slots, dtype=jnp.int32)
+        owners = slots_here[:, None] == target[None, :]
+        receive_index = jnp.sum(jnp.where(owners, row_rank[None, :], 0), axis=1)
+        placed = jnp.take(packed_sum, receive_index, axis=0, mode="clip")
+        return jnp.where(row_present[:, None, None], placed, 0.0)
+
+    row_sum = lax.cond(fits, packed, padded, local_rows)
     gradient = lax.psum_scatter(row_sum, "z", scatter_dimension=0, tiled=True)
     momentum_new = BETA * momentum[0] + gradient
     update = gradient + BETA * momentum_new

time: 348 us -> 334 us (0.960)
  blocking collectives: 96.2 us -> 0 us
  waiting for transfers between devices: 168 us -> 241 us
  starting transfers between devices: 11.3 us -> 15.6 us
    all_to_all x1 -> x0, blocking collectives: 96.2 us -> none  [on_device(): arrived = lax.all_to_all(outgoing, 'x', 0, 0, tiled=True)]
    all_to_all x0 -> x1, waiting for transfers between devices: none -> 69.2 us  [packed(): arrived = lax.all_to_all(outgoing, 'x', 0, 0, tiled=True)]
    all_to_all x0 -> x1, starting transfers between devices: none -> 5.24 us  [packed(): arrived = lax.all_to_all(outgoing, 'x', 0, 0, tiled=True)]
    gather x1 -> x3, local copies, waits for them, and re-layouts: 8.63 us -> 11 us  [the longest x1 8.19 us: packed(): outgoing = jnp.take(rows, send_index, axis=0, mode='clip')]
  transfers between devices with their start and end apart: 10 -> 11, of which waited for: 9 -> 10; matrix products, arithmetic and copies ran while one was open for 0% -> 0% of each run, Pallas kernels for 0% -> 0%
where the time goes in v8:
time: 334 us; the launch traced here: 333 us
  waiting for transfers between devices  241 us (72%)
  matrix products  27.2 us (8%)
  local copies, waits for them, and re-layouts  18.9 us (6%)
  starting transfers between devices  15.6 us (5%)
  other arithmetic  15.3 us (5%)
  between operations  14.9 us (4%)
    all_gather x1, waiting for transfers between devices, on_device(): every_slot = lax.all_gather(weights_low, ('x', 'z'), axis=0, tiled=True)  95 us
    all_to_all x1, waiting for transfers between devices, packed(): arrived = lax.all_to_all(outgoing, 'x', 0, 0, tiled=True)  69.2 us
    reduce_scatter x1, waiting for transfers between devices, on_device(): gradient = lax.psum_scatter(row_sum, 'z', scatter_dimension=0, tiled=True)  59.5 us
    dot_general x13, matrix products, matmul(): jnp.einsum('srt,stu->sru', left, right, precision=lax.Precision.HIGHEST,...  18.7 us
    ppermute x3, waiting for transfers between devices, own_sum(): lax.ppermute(jnp.take(quarters, chip ^ shift, axis=1, mode='clip'), 'own'...  8.38 us
    gather x1, local copies, waits for them, and re-layouts, packed(): outgoing = jnp.take(rows, send_index, axis=0, mode='clip')  8.19 us
  transfers between devices with their start and end apart: 11, of which 10 were waited for; matrix products, arithmetic and copies ran while one was open for 0% of the time, Pallas kernels for 0%

profile of v8, /device:TPU:1, one launch (start us, length us, event | category | flops | bytes accessed | tf_op | source)
XLA Modules:
  0.0 333.1 jit_solution(1108424695072661094)
XLA Ops:
  12.1 90.5 %conditional.1 = (pred[32,256,128]{2,1,0:T(8,128)(4,1)S(1)}, f32[32,256,128]{2,1,0:T(8,128)}, f32[]{:T(128)}, f32[]{:T(128)}) conditional(s32[]{:T(128)} %convert_element_type.30, (pred[32]{0:T(512)(128)(4,1)S(1)}, pred[128,64]{1,0:T(8,128)(4,1)S(1)}, s32[128,64]{1,0:T(8,128)S(1)}, bf16[64,256,128]{2,1,0:T(8,128)(2,1)}) %tuple.90, ...), branch_computations={%region_6.9_spmd, %region_9.14_spmd} | conditional | flops 7357312 | bytes 55621232 | solution.py:150
  12.3 8.2 %gather_fusion.1 = bf16[96,256,128]{2,1,0:T(8,128)(2,1)} fusion(bf16[64,256,128]{2,1,0:T(8,128)(2,1)} %get-tuple-element.91, s32[1024]{0:T(1024)S(1)} %pad_clamp_fusion.2), kind=kCustom, calls=%fused_computation.1 | custom fusion | bytes 12583296 | tf_op jit(solution)/shard_map/cond/branch_1_fun/jit(_take)/gather | solution.py:140
  20.5 5.2 %all-to-all-start.1 = ((bf16[4,24,256,128]{3,2,1,0:T(8,128)(2,1)}), bf16[4,24,256,128]{3,2,1,0:T(8,128)(2,1)}, u32[]{:S(2)}, u32[]{:S(2)}) async-start(bf16[4,24,256,128]{3,2,1,0:T(8,128)(2,1)} %bitcast.87), calls=%async_computation.1 | async-start | bytes 12582912 | tf_op jit(solution)/shard_map/cond/branch_1_fun/all_to_all | solution.py:142
  25.9 69.2 %all-to-all-done.1 = bf16[4,24,256,128]{3,2,1,0:T(8,128)(2,1)} async-done(((bf16[4,24,256,128]{3,2,1,0:T(8,128)(2,1)}), bf16[4,24,256,128]{3,2,1,0:T(8,128)(2,1)}, u32[]{:S(2)}, u32[]{:S(2)}) %all-to-all-start.1) | async-done | bytes 6291488 | tf_op jit(solution)/shard_map/cond/branch_1_fun/all_to_all | solution.py:142
  95.1 4.3 %convert_reduce_fusion.1 = f32[24,256,128]{2,1,0:T(8,128)S(1)} fusion(bf16[4,24,256,128]{3,2,1,0:T(8,128)(2,1)} %all-to-all-done.1), kind=kLoop, calls=%fused_computation.9 | loop fusion | flops 5505024 | bytes 9437184 | tf_op jit(solution)/shard_map/cond/branch_1_fun/reduce_sum | solution.py:143
  99.4 2.8 gather_fusion.2
  102.6 4.9 %broadcast_select_fusion = f32[32,256,128]{2,1,0:T(8,128)} fusion(pred[32,256,128]{2,1,0:T(8,128)(4,1)S(1)} %get-tuple-element.113, f32[32,256,128]{2,1,0:T(8,128)} %get-tuple-element.114, f32[]{:T(128)} %get-tuple-element.115), kind=kLoop, calls=%fused_computation.33 | loop fusion | flops 1048576 | bytes 9437188 | tf_op jit(solution)/shard_map/cond/branch_0_fun/jit(_where)/select_n | solution.py:134
  107.6 59.5 %reduce-scatter.2.cloned.1.call-done = f32[4,256,128]{2,1,0:T(8,128)} async-done(((f32[32,256,128]{2,1,0:T(8,128)}), f32[4,256,128]{2,1,0:T(8,128)}) %reduce-scatter.2.cloned.1.call-update) | async-done | bytes 524304 | tf_op jit(solution)/shard_map/reduce_scatter | solution.py:151
  167.1 2.3 fusion.14
  173.3 2.5 collective-permute-start.2
  176.8 5.0 %collective-permute-done.2 = f32[4,32,256]{2,1,0:T(8,128)S(1)} collective-permute-done((f32[4,32,256]{2,1,0:T(8,128)S(1)}, f32[4,32,256]{2,1,0:T(8,128)S(1)}, u32[]{:S(2)}, u32[]{:S(2)}) %collective-permute-start.2) | collective-permute-done | bytes 131104 | tf_op jit(solution)/shard_map/ppermute | solution.py:66
  181.8 2.5 collective-permute-done.3
  184.5 1.5 collective-permute-start.5
  186.0 2.3 collective-permute-start.6
  188.4 3.2 collective-permute-done.5
  191.6 2.6 collective-permute-done.6
  199.4 22.1 %while.18 = (s32[]{:T(128)}, f32[4,256,128]{2,1,0:T(8,128)S(1)}, f32[4,256,256]{2,1,0:T(8,128)S(1)}, s32[]{:T(128)}) while((s32[]{:T(128)}, f32[4,256,128]{2,1,0:T(8,128)S(1)}, f32[4,256,256]{2,1,0:T(8,128)S(1)}, s32[]{:T(128)}) %tuple.79), condition=%wide.region_17.18_spmd.clone, body=%wide.region_16.17_spmd.clone.sunk | while | flops 2820276224 | bytes 12320821 | solution.py:160
  200.6 1.9 fusion.55
  206.2 1.9 fusion.55
  211.7 1.9 fusion.55
  217.3 1.9 fusion.55
  222.8 2.0 fusion.24
  224.8 95.0 %all-gather.2.cloned.1.call-done = bf16[128,256,128]{2,1,0:T(8,128)(2,1)} async-done(((bf16[4,256,128]{2,1,0:T(8,128)(2,1)}), bf16[128,256,128]{2,1,0:T(8,128)(2,1)}) %all-gather.2.cloned.1.call-update) | async-done | bytes 8388624 | tf_op jit(solution)/shard_map/all_gather | solution.py:167
  319.8 6.5 %gather_fusion.4 = bf16[64,256,128]{2,1,0:T(8,128)(2,1)} fusion(bf16[128,256,128]{2,1,0:T(8,128)(2,1)} %all-gather.2.cloned.1.call-done, s32[1024]{0:T(1024)S(1)} %pad_clamp_fusion.3), kind=kCustom, calls=%fused_computation.4 | custom fusion | bytes 8388864 | tf_op jit(solution)/shard_map/jit(_take)/gather | solution.py:168
  (78 shorter events, 30.7 us)
Async XLA Ops:
  7.2 159.9 %reduce-scatter.2.cloned.1.call-start = ((), (), s32[]{:S(2)}) async-start(), calls=%async_computation.3 | async-start | bytes 4718592 | tf_op jit(solution)/shard_map/reduce_scatter | solution.py:151
  20.5 74.6 %all-to-all-start.1 = ((bf16[4,24,256,128]{3,2,1,0:T(8,128)(2,1)}), bf16[4,24,256,128]{3,2,1,0:T(8,128)(2,1)}, u32[]{:S(2)}, u32[]{:S(2)}) async-start(bf16[4,24,256,128]{3,2,1,0:T(8,128)(2,1)} %bitcast.87), calls=%async_computation.1 | async-start | bytes 12582912 | tf_op jit(solution)/shard_map/cond/branch_1_fun/all_to_all | solution.py:142
  107.5 59.6 %copy-start = (f32[1,4,256,128]{3,2,1,0:T(8,128)S(1)}, f32[1,4,256,128]{3,2,1,0:T(8,128)}, u32[]{:S(2)}) copy-start(f32[1,4,256,128]{3,2,1,0:T(8,128)} %param.10) | copy-start | bytes 1572868
  107.5 212.3 %all-gather.2.cloned.1.call-start = ((), (), s32[]{:S(2)}) async-start(), calls=%async_computation.4 | async-start | bytes 8650752 | tf_op jit(solution)/shard_map/all_gather | solution.py:167
  169.5 2.4 collective-permute-start
  172.0 26.5 %copy-start.1 = (f32[4,256,128]{2,1,0:T(8,128)S(1)}, f32[4,256,128]{2,1,0:T(8,128)}, u32[]{:S(2)}) copy-start(f32[4,256,128]{2,1,0:T(8,128)} %reduce-scatter.2.cloned.1.call-done) | copy-start | bytes 1572868
  172.0 4.8 %collective-permute-start.1 = (f32[4,32,256]{2,1,0:T(8,128)S(1)}, f32[4,32,256]{2,1,0:T(8,128)S(1)}, u32[]{:S(2)}, u32[]{:S(2)}) collective-permute-start(f32[4,32,256]{2,1,0:T(8,128)S(1)} %get-tuple-element.258), channel_id=1, source_target_pairs={{0,2},{1,3},{2,0},{3,1},{4,6},{5,7},{6,4},{7,5},{8,10},{9,11},{10,... | collective-permute-start | bytes 393224 | tf_op jit(solution)/shard_map/ppermute | solution.py:66
  173.3 8.5 %collective-permute-start.2 = (f32[4,32,256]{2,1,0:T(8,128)S(1)}, f32[4,32,256]{2,1,0:T(8,128)S(1)}, u32[]{:S(2)}, u32[]{:S(2)}) collective-permute-start(f32[4,32,256]{2,1,0:T(8,128)S(1)} %get-tuple-element.260), channel_id=1, source_target_pairs={{0,4},{1,5},{2,6},{3,7},{4,0},{5,1},{6,2},{7,3},{8,12},{9,13},{10,... | collective-permute-start | bytes 393224 | tf_op jit(solution)/shard_map/ppermute | solution.py:66
  175.7 8.6 %collective-permute-start.3 = (f32[4,32,256]{2,1,0:T(8,128)S(1)}, f32[4,32,256]{2,1,0:T(8,128)S(1)}, u32[]{:S(2)}, u32[]{:S(2)}) collective-permute-start(f32[4,32,256]{2,1,0:T(8,128)S(1)} %get-tuple-element.259), channel_id=1, source_target_pairs={{0,6},{1,7},{2,4},{3,5},{4,2},{5,3},{6,0},{7,1},{8,14},{9,15},{10,... | collective-permute-start | bytes 393224 | tf_op jit(solution)/shard_map/ppermute | solution.py:66
  184.4 4.0 %collective-permute-start.4 = (f32[4,32,256]{2,1,0:T(8,128)S(1)}, f32[4,32,256]{2,1,0:T(8,128)S(1)}, u32[]{:S(2)}, u32[]{:S(2)}) collective-permute-start(f32[4,32,256]{2,1,0:T(8,128)S(1)} %fusion.16), channel_id=1, source_target_pairs={{0,2},{1,3},{2,0},{3,1},{4,6},{5,7},{6,4},{7,5},{8,10},{9,11},{10,... | collective-permute-start | bytes 393224 | tf_op jit(solution)/shard_map/ppermute | solution.py:72
  184.5 7.1 %collective-permute-start.5 = (f32[4,32,256]{2,1,0:T(8,128)S(1)}, f32[4,32,256]{2,1,0:T(8,128)S(1)}, u32[]{:S(2)}, u32[]{:S(2)}) collective-permute-start(f32[4,32,256]{2,1,0:T(8,128)S(1)} %fusion.16), channel_id=1, source_target_pairs={{0,4},{1,5},{2,6},{3,7},{4,0},{5,1},{6,2},{7,3},{8,12},{9,13},{10,... | collective-permute-start | bytes 393224 | tf_op jit(solution)/shard_map/ppermute | solution.py:72
  186.0 8.1 %collective-permute-start.6 = (f32[4,32,256]{2,1,0:T(8,128)S(1)}, f32[4,32,256]{2,1,0:T(8,128)S(1)}, u32[]{:S(2)}, u32[]{:S(2)}) collective-permute-start(f32[4,32,256]{2,1,0:T(8,128)S(1)} %fusion.16), channel_id=1, source_target_pairs={{0,6},{1,7},{2,4},{3,5},{4,2},{5,3},{6,0},{7,1},{8,14},{9,15},{10,... | collective-permute-start | bytes 393224 | tf_op jit(solution)/shard_map/ppermute | solution.py:72
  194.9 3.1 collective-permute-start.7
  199.3 23.4 %copy-start.2 = (f32[1,4,256,128]{3,2,1,0:T(8,128)S(1)}, f32[1,4,256,128]{3,2,1,0:T(8,128)}, u32[]{:S(2)}) copy-start(f32[1,4,256,128]{3,2,1,0:T(8,128)} %param.11) | copy-start | bytes 1572868
Sparse Core Ops, SparseCore 0:
  107.6 59.3 reduce-scatter.1
  224.9 94.8 all-gather.1

commit v9 on v8

--- a/solution.py
+++ b/solution.py
@@ -141,11 +141,12 @@
         outgoing = outgoing.reshape((row_count, width) + outgoing.shape[1:])
         arrived = lax.all_to_all(outgoing, "x", 0, 0, tiled=True)
         packed_sum = jnp.sum(arrived.astype(jnp.float32), axis=0)
+        packed_sum = jnp.concatenate([packed_sum, jnp.zeros_like(packed_sum[:1])], axis=0)
         slots_here = here * row_slots + jnp.arange(row_slots, dtype=jnp.int32)
         owners = slots_here[:, None] == target[None, :]
         receive_index = jnp.sum(jnp.where(owners, row_rank[None, :], 0), axis=1)
-        placed = jnp.take(packed_sum, receive_index, axis=0, mode="clip")
-        return jnp.where(row_present[:, None, None], placed, 0.0)
+        receive_index = jnp.where(row_present, receive_index, width)
+        return jnp.take(packed_sum, receive_index, axis=0, mode="clip")
 
     row_sum = lax.cond(fits, packed, padded, local_rows)
     gradient = lax.psum_scatter(row_sum, "z", scatter_dimension=0, tiled=True)

time: 334 us -> 329 us (0.985)
  other arithmetic: 15.3 us -> 10.4 us
    select_n x1, other arithmetic: 4.91 us -> 0.01 us  [packed(): receive_index = jnp.where(row_present, receive_index, width)]
where the time goes in v9:
time: 329 us; the launch traced here: 328 us
  waiting for transfers between devices  241 us (73%)
  matrix products  27.2 us (8%)
  local copies, waits for them, and re-layouts  18.9 us (6%)
  starting transfers between devices  15.5 us (5%)
  between operations  14.9 us (5%)
  other arithmetic  10.4 us (3%)
    all_gather x1, waiting for transfers between devices, on_device(): every_slot = lax.all_gather(weights_low, ('x', 'z'), axis=0, tiled=True)  95 us
    all_to_all x1, waiting for transfers between devices, packed(): arrived = lax.all_to_all(outgoing, 'x', 0, 0, tiled=True)  69.2 us
    reduce_scatter x1, waiting for transfers between devices, on_device(): gradient = lax.psum_scatter(row_sum, 'z', scatter_dimension=0, tiled=True)  59.5 us
    dot_general x13, matrix products, matmul(): jnp.einsum('srt,stu->sru', left, right, precision=lax.Precision.HIGHEST,...  18.7 us
    ppermute x3, waiting for transfers between devices, own_sum(): lax.ppermute(jnp.take(quarters, chip ^ shift, axis=1, mode='clip'), 'own'...  8.39 us
    gather x1, local copies, waits for them, and re-layouts, packed(): outgoing = jnp.take(rows, send_index, axis=0, mode='clip')  8.2 us
  transfers between devices with their start and end apart: 11, of which 10 were waited for; matrix products, arithmetic and copies ran while one was open for 0% of the time, Pallas kernels for 0%

profile of v9, /device:TPU:1, one launch (start us, length us, event | category | flops | bytes accessed | tf_op | source)
XLA Modules:
  0.0 328.2 jit_solution(11078227924505114512)
XLA Ops:
  12.1 90.6 %conditional.1 = (f32[32,256,128]{2,1,0:T(8,128)}) conditional(s32[]{:T(128)} %convert_element_type.30, (pred[32]{0:T(512)(128)(4,1)S(1)}, pred[128,64]{1,0:T(8,128)(4,1)S(1)}, s32[128,64]{1,0:T(8,128)S(1)}, bf16[64,256,128]{2,1,0:T(8,128)(2,1)}) %tuple.81, (s32[64]{0:T(128)S(1)}, s32[64]{0:T(128)S(1)}, s32[]{:T(128)}, s32[64,4]{1,0:T(8,128)S(1)}, ...), branch_computations={%region_6.9_spmd, %region_9.14_spmd} | conditional | flops 8405888 | bytes 55722336 | solution.py:151
  12.3 8.2 %gather_fusion.1 = bf16[96,256,128]{2,1,0:T(8,128)(2,1)} fusion(bf16[64,256,128]{2,1,0:T(8,128)(2,1)} %get-tuple-element.91, s32[1024]{0:T(1024)S(1)} %pad_clamp_fusion.2), kind=kCustom, calls=%fused_computation.1 | custom fusion | bytes 12583296 | tf_op jit(solution)/shard_map/cond/branch_1_fun/jit(_take)/gather | solution.py:140
  20.5 5.2 %all-to-all-start.1 = ((bf16[4,24,256,128]{3,2,1,0:T(8,128)(2,1)}), bf16[4,24,256,128]{3,2,1,0:T(8,128)(2,1)}, u32[]{:S(2)}, u32[]{:S(2)}) async-start(bf16[4,24,256,128]{3,2,1,0:T(8,128)(2,1)} %bitcast.87), calls=%async_computation.1 | async-start | bytes 12582912 | tf_op jit(solution)/shard_map/cond/branch_1_fun/all_to_all | solution.py:142
  26.0 69.2 %all-to-all-done.1 = bf16[4,24,256,128]{3,2,1,0:T(8,128)(2,1)} async-done(((bf16[4,24,256,128]{3,2,1,0:T(8,128)(2,1)}), bf16[4,24,256,128]{3,2,1,0:T(8,128)(2,1)}, u32[]{:S(2)}, u32[]{:S(2)}) %all-to-all-start.1) | async-done | bytes 6291488 | tf_op jit(solution)/shard_map/cond/branch_1_fun/all_to_all | solution.py:142
  95.1 4.3 %convert_reduce_fusion.1 = f32[24,256,128]{2,1,0:T(8,128)S(1)} fusion(bf16[4,24,256,128]{3,2,1,0:T(8,128)(2,1)} %all-to-all-done.1), kind=kLoop, calls=%fused_computation.10 | loop fusion | flops 5505024 | bytes 9437184 | tf_op jit(solution)/shard_map/cond/branch_1_fun/reduce_sum | solution.py:143
  99.8 2.8 gather_fusion.2
  102.7 59.5 %reduce-scatter.2.cloned.1.call-done = f32[4,256,128]{2,1,0:T(8,128)} async-done(((f32[32,256,128]{2,1,0:T(8,128)}), f32[4,256,128]{2,1,0:T(8,128)}) %reduce-scatter.2.cloned.1.call-update) | async-done | bytes 524304 | tf_op jit(solution)/shard_map/reduce_scatter | solution.py:152
  162.2 2.3 fusion.14
  165.4 1.5 collective-permute-done
  168.4 2.5 collective-permute-start.2
  171.9 5.0 %collective-permute-done.2 = f32[4,32,256]{2,1,0:T(8,128)S(1)} collective-permute-done((f32[4,32,256]{2,1,0:T(8,128)S(1)}, f32[4,32,256]{2,1,0:T(8,128)S(1)}, u32[]{:S(2)}, u32[]{:S(2)}) %collective-permute-start.2) | collective-permute-done | bytes 131104 | tf_op jit(solution)/shard_map/ppermute | solution.py:66
  176.9 2.5 collective-permute-done.3
  179.8 1.5 collective-permute-start.5
  181.3 2.3 collective-permute-start.6
  183.6 3.2 collective-permute-done.5
  186.9 2.6 collective-permute-done.6
  194.4 22.1 %while.18 = (s32[]{:T(128)}, f32[4,256,128]{2,1,0:T(8,128)S(1)}, f32[4,256,256]{2,1,0:T(8,128)S(1)}, s32[]{:T(128)}) while((s32[]{:T(128)}, f32[4,256,128]{2,1,0:T(8,128)S(1)}, f32[4,256,256]{2,1,0:T(8,128)S(1)}, s32[]{:T(128)}) %tuple.72), condition=%wide.region_17.18_spmd.clone, body=%wide.region_16.17_spmd.clone.sunk | while | flops 2820276224 | bytes 12320821 | solution.py:161
  195.7 1.9 fusion.55
  201.2 1.9 fusion.55
  206.8 1.9 fusion.55
  212.3 1.9 fusion.55
  217.8 2.0 fusion.24
  219.8 95.0 %all-gather.2.cloned.1.call-done = bf16[128,256,128]{2,1,0:T(8,128)(2,1)} async-done(((bf16[4,256,128]{2,1,0:T(8,128)(2,1)}), bf16[128,256,128]{2,1,0:T(8,128)(2,1)}) %all-gather.2.cloned.1.call-update) | async-done | bytes 8388624 | tf_op jit(solution)/shard_map/all_gather | solution.py:168
  314.9 6.5 %gather_fusion.4 = bf16[64,256,128]{2,1,0:T(8,128)(2,1)} fusion(bf16[128,256,128]{2,1,0:T(8,128)(2,1)} %all-gather.2.cloned.1.call-done, s32[1024]{0:T(1024)S(1)} %pad_clamp_fusion.3), kind=kCustom, calls=%fused_computation.4 | custom fusion | bytes 8388864 | tf_op jit(solution)/shard_map/jit(_take)/gather | solution.py:169
  (78 shorter events, 29.1 us)
Async XLA Ops:
  7.2 155.0 %reduce-scatter.2.cloned.1.call-start = ((), (), s32[]{:S(2)}) async-start(), calls=%async_computation.3 | async-start | bytes 4718592 | tf_op jit(solution)/shard_map/reduce_scatter | solution.py:152
  20.5 74.6 %all-to-all-start.1 = ((bf16[4,24,256,128]{3,2,1,0:T(8,128)(2,1)}), bf16[4,24,256,128]{3,2,1,0:T(8,128)(2,1)}, u32[]{:S(2)}, u32[]{:S(2)}) async-start(bf16[4,24,256,128]{3,2,1,0:T(8,128)(2,1)} %bitcast.87), calls=%async_computation.1 | async-start | bytes 12582912 | tf_op jit(solution)/shard_map/cond/branch_1_fun/all_to_all | solution.py:142
  102.6 59.6 %copy-start = (f32[1,4,256,128]{3,2,1,0:T(8,128)S(1)}, f32[1,4,256,128]{3,2,1,0:T(8,128)}, u32[]{:S(2)}) copy-start(f32[1,4,256,128]{3,2,1,0:T(8,128)} %param.10) | copy-start | bytes 1572868
  102.6 212.3 %all-gather.2.cloned.1.call-start = ((), (), s32[]{:S(2)}) async-start(), calls=%async_computation.4 | async-start | bytes 8650752 | tf_op jit(solution)/shard_map/all_gather | solution.py:168
  164.6 2.4 collective-permute-start
  167.1 26.4 %copy-start.1 = (f32[4,256,128]{2,1,0:T(8,128)S(1)}, f32[4,256,128]{2,1,0:T(8,128)}, u32[]{:S(2)}) copy-start(f32[4,256,128]{2,1,0:T(8,128)} %reduce-scatter.2.cloned.1.call-done) | copy-start | bytes 1572868
  167.1 4.8 %collective-permute-start.1 = (f32[4,32,256]{2,1,0:T(8,128)S(1)}, f32[4,32,256]{2,1,0:T(8,128)S(1)}, u32[]{:S(2)}, u32[]{:S(2)}) collective-permute-start(f32[4,32,256]{2,1,0:T(8,128)S(1)} %get-tuple-element.238), channel_id=1, source_target_pairs={{0,2},{1,3},{2,0},{3,1},{4,6},{5,7},{6,4},{7,5},{8,10},{9,11},{10,... | collective-permute-start | bytes 393224 | tf_op jit(solution)/shard_map/ppermute | solution.py:66
  168.4 8.5 %collective-permute-start.2 = (f32[4,32,256]{2,1,0:T(8,128)S(1)}, f32[4,32,256]{2,1,0:T(8,128)S(1)}, u32[]{:S(2)}, u32[]{:S(2)}) collective-permute-start(f32[4,32,256]{2,1,0:T(8,128)S(1)} %get-tuple-element.240), channel_id=1, source_target_pairs={{0,4},{1,5},{2,6},{3,7},{4,0},{5,1},{6,2},{7,3},{8,12},{9,13},{10,... | collective-permute-start | bytes 393224 | tf_op jit(solution)/shard_map/ppermute | solution.py:66
  170.9 8.6 %collective-permute-start.3 = (f32[4,32,256]{2,1,0:T(8,128)S(1)}, f32[4,32,256]{2,1,0:T(8,128)S(1)}, u32[]{:S(2)}, u32[]{:S(2)}) collective-permute-start(f32[4,32,256]{2,1,0:T(8,128)S(1)} %get-tuple-element.239), channel_id=1, source_target_pairs={{0,6},{1,7},{2,4},{3,5},{4,2},{5,3},{6,0},{7,1},{8,14},{9,15},{10,... | collective-permute-start | bytes 393224 | tf_op jit(solution)/shard_map/ppermute | solution.py:66
  179.5 4.1 %collective-permute-start.4 = (f32[4,32,256]{2,1,0:T(8,128)S(1)}, f32[4,32,256]{2,1,0:T(8,128)S(1)}, u32[]{:S(2)}, u32[]{:S(2)}) collective-permute-start(f32[4,32,256]{2,1,0:T(8,128)S(1)} %fusion.16), channel_id=1, source_target_pairs={{0,2},{1,3},{2,0},{3,1},{4,6},{5,7},{6,4},{7,5},{8,10},{9,11},{10,... | collective-permute-start | bytes 393224 | tf_op jit(solution)/shard_map/ppermute | solution.py:72
  179.8 7.1 %collective-permute-start.5 = (f32[4,32,256]{2,1,0:T(8,128)S(1)}, f32[4,32,256]{2,1,0:T(8,128)S(1)}, u32[]{:S(2)}, u32[]{:S(2)}) collective-permute-start(f32[4,32,256]{2,1,0:T(8,128)S(1)} %fusion.16), channel_id=1, source_target_pairs={{0,4},{1,5},{2,6},{3,7},{4,0},{5,1},{6,2},{7,3},{8,12},{9,13},{10,... | collective-permute-start | bytes 393224 | tf_op jit(solution)/shard_map/ppermute | solution.py:72
  181.3 8.2 %collective-permute-start.6 = (f32[4,32,256]{2,1,0:T(8,128)S(1)}, f32[4,32,256]{2,1,0:T(8,128)S(1)}, u32[]{:S(2)}, u32[]{:S(2)}) collective-permute-start(f32[4,32,256]{2,1,0:T(8,128)S(1)} %fusion.16), channel_id=1, source_target_pairs={{0,6},{1,7},{2,4},{3,5},{4,2},{5,3},{6,0},{7,1},{8,14},{9,15},{10,... | collective-permute-start | bytes 393224 | tf_op jit(solution)/shard_map/ppermute | solution.py:72
  190.1 2.8 collective-permute-start.7
  194.4 23.4 %copy-start.2 = (f32[1,4,256,128]{3,2,1,0:T(8,128)S(1)}, f32[1,4,256,128]{3,2,1,0:T(8,128)}, u32[]{:S(2)}) copy-start(f32[1,4,256,128]{3,2,1,0:T(8,128)} %param.11) | copy-start | bytes 1572868
Sparse Core Ops, SparseCore 0:
  102.8 59.3 reduce-scatter.1
  220.0 94.8 all-gather.1

commit v10 on v9

--- a/solution.py
+++ b/solution.py
@@ -45,6 +45,60 @@
         precision=lax.Precision.HIGHEST,
         preferred_element_type=jnp.float32,
     )
+
+
+def own_sum(total):
+    size = lax.axis_size("own")
+    index = lax.axis_index("own")
+    rows = total.shape[1]
+    core_pairs = [(i, i ^ 1) for i in range(size)]
+    high = (index & 1) != 0
+    lower, upper = total[:, : rows // 2], total[:, rows // 2 :]
+    keep = jnp.where(high, upper, lower)
+    total = keep + lax.ppermute(jnp.where(high, lower, upper), "own", core_pairs)
+    chips = size // 2
+    chip = index // 2
+    piece = total.shape[1] // chips
+    quarters = total.reshape(total.shape[0], chips, piece, total.shape[2])
+    summed = jnp.take(quarters, chip, axis=1, mode="clip")
+    for shift in range(1, chips):
+        pairs = [(i, i ^ (2 * shift)) for i in range(size)]
+        summed = summed + lax.ppermute(
+            jnp.take(quarters, chip ^ shift, axis=1, mode="clip"), "own", pairs
+        )
+    arrived = [summed]
+    for shift in range(1, chips):
+        pairs = [(i, i ^ (2 * shift)) for i in range(size)]
+        arrived.append(lax.ppermute(summed, "own", pairs))
+    arrived = jnp.stack(arrived, axis=1)
+    order = jnp.arange(chips, dtype=jnp.int32) ^ chip
+    total = jnp.take(arrived, order, axis=1, mode="clip").reshape(total.shape)
+    other = lax.ppermute(total, "own", core_pairs)
+    return jnp.where(high, jnp.concatenate([other, total], axis=1), jnp.concatenate([total, other], axis=1))
+
+
+def gram_total(values):
+    return own_sum(local_gram(values))
+
+
+def matmul(left, right):
+    return jnp.einsum(
+        "srt,stu->sru",
+        left,
+        right,
+        precision=lax.Precision.HIGHEST,
+        preferred_element_type=jnp.float32,
+    )
+
+
+def newton_turn(ortho, gram, eye, next_gram):
+    square = matmul(gram, gram)
+    step = COEF_A * eye + COEF_B * gram + COEF_C * square
+    if not next_gram:
+        return matmul(step, ortho), gram
+    width = ortho.shape[2]
+    both = matmul(step, jnp.concatenate([ortho, matmul(gram, step)], axis=2))
+    return both[:, :, :width], both[:, :, width:]
 
 
 def own_sum(total):

time: 329 us -> 329 us (level)
  no operation moved by 1% of the time
where the time goes in v10:
time: 329 us; the launch traced here: 328 us
  waiting for transfers between devices  241 us (73%)
  matrix products  27.2 us (8%)
  local copies, waits for them, and re-layouts  18.9 us (6%)
  starting transfers between devices  15.5 us (5%)
  between operations  14.9 us (5%)
  other arithmetic  10.4 us (3%)
    all_gather x1, waiting for transfers between devices, on_device(): every_slot = lax.all_gather(weights_low, ('x', 'z'), axis=0, tiled=True)  95 us
    all_to_all x1, waiting for transfers between devices, packed(): arrived = lax.all_to_all(outgoing, 'x', 0, 0, tiled=True)  69.2 us
    reduce_scatter x1, waiting for transfers between devices, on_device(): gradient = lax.psum_scatter(row_sum, 'z', scatter_dimension=0, tiled=True)  59.5 us
    dot_general x13, matrix products, matmul(): jnp.einsum('srt,stu->sru', left, right, precision=lax.Precision.HIGHEST,...  18.7 us
    ppermute x3, waiting for transfers between devices, own_sum(): lax.ppermute(jnp.take(quarters, chip ^ shift, axis=1, mode='clip'), 'own'...  8.39 us
    gather x1, local copies, waits for them, and re-layouts, packed(): outgoing = jnp.take(rows, send_index, axis=0, mode='clip')  8.2 us
  transfers between devices with their start and end apart: 11, of which 10 were waited for; matrix products, arithmetic and copies ran while one was open for 0% of the time, Pallas kernels for 0%

profile of v10, /device:TPU:1, one launch (start us, length us, event | category | flops | bytes accessed | tf_op | source)
XLA Modules:
  0.0 328.2 jit_solution(11078227924505114512)
XLA Ops:
  12.1 90.6 %conditional.1 = (f32[32,256,128]{2,1,0:T(8,128)}) conditional(s32[]{:T(128)} %convert_element_type.30, (pred[32]{0:T(512)(128)(4,1)S(1)}, pred[128,64]{1,0:T(8,128)(4,1)S(1)}, s32[128,64]{1,0:T(8,128)S(1)}, bf16[64,256,128]{2,1,0:T(8,128)(2,1)}) %tuple.81, (s32[64]{0:T(128)S(1)}, s32[64]{0:T(128)S(1)}, s32[]{:T(128)}, s32[64,4]{1,0:T(8,128)S(1)}, ...), branch_computations={%region_6.9_spmd, %region_9.14_spmd} | conditional | flops 8405888 | bytes 55722336 | solution.py:205
  12.3 8.2 %gather_fusion.1 = bf16[96,256,128]{2,1,0:T(8,128)(2,1)} fusion(bf16[64,256,128]{2,1,0:T(8,128)(2,1)} %get-tuple-element.91, s32[1024]{0:T(1024)S(1)} %pad_clamp_fusion.2), kind=kCustom, calls=%fused_computation.1 | custom fusion | bytes 12583296 | tf_op jit(solution)/shard_map/cond/branch_1_fun/jit(_take)/gather | solution.py:194
  20.5 5.2 %all-to-all-start.1 = ((bf16[4,24,256,128]{3,2,1,0:T(8,128)(2,1)}), bf16[4,24,256,128]{3,2,1,0:T(8,128)(2,1)}, u32[]{:S(2)}, u32[]{:S(2)}) async-start(bf16[4,24,256,128]{3,2,1,0:T(8,128)(2,1)} %bitcast.87), calls=%async_computation.1 | async-start | bytes 12582912 | tf_op jit(solution)/shard_map/cond/branch_1_fun/all_to_all | solution.py:196
  26.0 69.2 %all-to-all-done.1 = bf16[4,24,256,128]{3,2,1,0:T(8,128)(2,1)} async-done(((bf16[4,24,256,128]{3,2,1,0:T(8,128)(2,1)}), bf16[4,24,256,128]{3,2,1,0:T(8,128)(2,1)}, u32[]{:S(2)}, u32[]{:S(2)}) %all-to-all-start.1) | async-done | bytes 6291488 | tf_op jit(solution)/shard_map/cond/branch_1_fun/all_to_all | solution.py:196
  95.1 4.3 %convert_reduce_fusion.1 = f32[24,256,128]{2,1,0:T(8,128)S(1)} fusion(bf16[4,24,256,128]{3,2,1,0:T(8,128)(2,1)} %all-to-all-done.1), kind=kLoop, calls=%fused_computation.10 | loop fusion | flops 5505024 | bytes 9437184 | tf_op jit(solution)/shard_map/cond/branch_1_fun/reduce_sum | solution.py:197
  99.8 2.8 gather_fusion.2
  102.7 59.5 %reduce-scatter.2.cloned.1.call-done = f32[4,256,128]{2,1,0:T(8,128)} async-done(((f32[32,256,128]{2,1,0:T(8,128)}), f32[4,256,128]{2,1,0:T(8,128)}) %reduce-scatter.2.cloned.1.call-update) | async-done | bytes 524304 | tf_op jit(solution)/shard_map/reduce_scatter | solution.py:206
  162.2 2.3 fusion.14
  165.4 1.5 collective-permute-done
  168.4 2.5 collective-permute-start.2
  171.9 5.0 %collective-permute-done.2 = f32[4,32,256]{2,1,0:T(8,128)S(1)} collective-permute-done((f32[4,32,256]{2,1,0:T(8,128)S(1)}, f32[4,32,256]{2,1,0:T(8,128)S(1)}, u32[]{:S(2)}, u32[]{:S(2)}) %collective-permute-start.2) | collective-permute-done | bytes 131104 | tf_op jit(solution)/shard_map/ppermute | solution.py:120
  176.9 2.5 collective-permute-done.3
  179.8 1.5 collective-permute-start.5
  181.3 2.3 collective-permute-start.6
  183.6 3.2 collective-permute-done.5
  186.9 2.6 collective-permute-done.6
  194.4 22.1 %while.18 = (s32[]{:T(128)}, f32[4,256,128]{2,1,0:T(8,128)S(1)}, f32[4,256,256]{2,1,0:T(8,128)S(1)}, s32[]{:T(128)}) while((s32[]{:T(128)}, f32[4,256,128]{2,1,0:T(8,128)S(1)}, f32[4,256,256]{2,1,0:T(8,128)S(1)}, s32[]{:T(128)}) %tuple.72), condition=%wide.region_17.18_spmd.clone, body=%wide.region_16.17_spmd.clone.sunk | while | flops 2820276224 | bytes 12320821 | solution.py:215
  195.7 1.9 fusion.55
  201.2 1.9 fusion.55
  206.8 1.9 fusion.55
  212.3 1.9 fusion.55
  217.8 2.0 fusion.24
  219.8 95.0 %all-gather.2.cloned.1.call-done = bf16[128,256,128]{2,1,0:T(8,128)(2,1)} async-done(((bf16[4,256,128]{2,1,0:T(8,128)(2,1)}), bf16[128,256,128]{2,1,0:T(8,128)(2,1)}) %all-gather.2.cloned.1.call-update) | async-done | bytes 8388624 | tf_op jit(solution)/shard_map/all_gather | solution.py:222
  314.9 6.5 %gather_fusion.4 = bf16[64,256,128]{2,1,0:T(8,128)(2,1)} fusion(bf16[128,256,128]{2,1,0:T(8,128)(2,1)} %all-gather.2.cloned.1.call-done, s32[1024]{0:T(1024)S(1)} %pad_clamp_fusion.3), kind=kCustom, calls=%fused_computation.4 | custom fusion | bytes 8388864 | tf_op jit(solution)/shard_map/jit(_take)/gather | solution.py:223
  (78 shorter events, 29.1 us)
Async XLA Ops:
  7.2 155.0 %reduce-scatter.2.cloned.1.call-start = ((), (), s32[]{:S(2)}) async-start(), calls=%async_computation.3 | async-start | bytes 4718592 | tf_op jit(solution)/shard_map/reduce_scatter | solution.py:206
  20.5 74.6 %all-to-all-start.1 = ((bf16[4,24,256,128]{3,2,1,0:T(8,128)(2,1)}), bf16[4,24,256,128]{3,2,1,0:T(8,128)(2,1)}, u32[]{:S(2)}, u32[]{:S(2)}) async-start(bf16[4,24,256,128]{3,2,1,0:T(8,128)(2,1)} %bitcast.87), calls=%async_computation.1 | async-start | bytes 12582912 | tf_op jit(solution)/shard_map/cond/branch_1_fun/all_to_all | solution.py:196
  102.6 59.6 %copy-start = (f32[1,4,256,128]{3,2,1,0:T(8,128)S(1)}, f32[1,4,256,128]{3,2,1,0:T(8,128)}, u32[]{:S(2)}) copy-start(f32[1,4,256,128]{3,2,1,0:T(8,128)} %param.10) | copy-start | bytes 1572868
  102.6 212.3 %all-gather.2.cloned.1.call-start = ((), (), s32[]{:S(2)}) async-start(), calls=%async_computation.4 | async-start | bytes 8650752 | tf_op jit(solution)/shard_map/all_gather | solution.py:222
  164.6 2.4 collective-permute-start
  167.1 26.4 %copy-start.1 = (f32[4,256,128]{2,1,0:T(8,128)S(1)}, f32[4,256,128]{2,1,0:T(8,128)}, u32[]{:S(2)}) copy-start(f32[4,256,128]{2,1,0:T(8,128)} %reduce-scatter.2.cloned.1.call-done) | copy-start | bytes 1572868
  167.1 4.8 %collective-permute-start.1 = (f32[4,32,256]{2,1,0:T(8,128)S(1)}, f32[4,32,256]{2,1,0:T(8,128)S(1)}, u32[]{:S(2)}, u32[]{:S(2)}) collective-permute-start(f32[4,32,256]{2,1,0:T(8,128)S(1)} %get-tuple-element.238), channel_id=1, source_target_pairs={{0,2},{1,3},{2,0},{3,1},{4,6},{5,7},{6,4},{7,5},{8,10},{9,11},{10,... | collective-permute-start | bytes 393224 | tf_op jit(solution)/shard_map/ppermute | solution.py:120
  168.4 8.5 %collective-permute-start.2 = (f32[4,32,256]{2,1,0:T(8,128)S(1)}, f32[4,32,256]{2,1,0:T(8,128)S(1)}, u32[]{:S(2)}, u32[]{:S(2)}) collective-permute-start(f32[4,32,256]{2,1,0:T(8,128)S(1)} %get-tuple-element.240), channel_id=1, source_target_pairs={{0,4},{1,5},{2,6},{3,7},{4,0},{5,1},{6,2},{7,3},{8,12},{9,13},{10,... | collective-permute-start | bytes 393224 | tf_op jit(solution)/shard_map/ppermute | solution.py:120
  170.9 8.6 %collective-permute-start.3 = (f32[4,32,256]{2,1,0:T(8,128)S(1)}, f32[4,32,256]{2,1,0:T(8,128)S(1)}, u32[]{:S(2)}, u32[]{:S(2)}) collective-permute-start(f32[4,32,256]{2,1,0:T(8,128)S(1)} %get-tuple-element.239), channel_id=1, source_target_pairs={{0,6},{1,7},{2,4},{3,5},{4,2},{5,3},{6,0},{7,1},{8,14},{9,15},{10,... | collective-permute-start | bytes 393224 | tf_op jit(solution)/shard_map/ppermute | solution.py:120
  179.5 4.1 %collective-permute-start.4 = (f32[4,32,256]{2,1,0:T(8,128)S(1)}, f32[4,32,256]{2,1,0:T(8,128)S(1)}, u32[]{:S(2)}, u32[]{:S(2)}) collective-permute-start(f32[4,32,256]{2,1,0:T(8,128)S(1)} %fusion.16), channel_id=1, source_target_pairs={{0,2},{1,3},{2,0},{3,1},{4,6},{5,7},{6,4},{7,5},{8,10},{9,11},{10,... | collective-permute-start | bytes 393224 | tf_op jit(solution)/shard_map/ppermute | solution.py:126
  179.8 7.1 %collective-permute-start.5 = (f32[4,32,256]{2,1,0:T(8,128)S(1)}, f32[4,32,256]{2,1,0:T(8,128)S(1)}, u32[]{:S(2)}, u32[]{:S(2)}) collective-permute-start(f32[4,32,256]{2,1,0:T(8,128)S(1)} %fusion.16), channel_id=1, source_target_pairs={{0,4},{1,5},{2,6},{3,7},{4,0},{5,1},{6,2},{7,3},{8,12},{9,13},{10,... | collective-permute-start | bytes 393224 | tf_op jit(solution)/shard_map/ppermute | solution.py:126
  181.3 8.2 %collective-permute-start.6 = (f32[4,32,256]{2,1,0:T(8,128)S(1)}, f32[4,32,256]{2,1,0:T(8,128)S(1)}, u32[]{:S(2)}, u32[]{:S(2)}) collective-permute-start(f32[4,32,256]{2,1,0:T(8,128)S(1)} %fusion.16), channel_id=1, source_target_pairs={{0,6},{1,7},{2,4},{3,5},{4,2},{5,3},{6,0},{7,1},{8,14},{9,15},{10,... | collective-permute-start | bytes 393224 | tf_op jit(solution)/shard_map/ppermute | solution.py:126
  190.1 2.8 collective-permute-start.7
  194.4 23.4 %copy-start.2 = (f32[1,4,256,128]{3,2,1,0:T(8,128)S(1)}, f32[1,4,256,128]{3,2,1,0:T(8,128)}, u32[]{:S(2)}) copy-start(f32[1,4,256,128]{3,2,1,0:T(8,128)} %param.11) | copy-start | bytes 1572868
Sparse Core Ops, SparseCore 0:
  102.8 59.3 reduce-scatter.1
  220.0 94.8 all-gather.1

commit v11 on v9

--- a/solution.py
+++ b/solution.py
@@ -119,7 +119,7 @@
     present, source = slot_sources(target, group_count * slot_count, block_count)
     row_count = lax.axis_size("x")
     row_slots = group_count * slot_count // row_count
-    width = row_slots * 3 // 4
+    width = row_slots * 11 // 16
     row_of = target // row_slots
     row_hot = (row_of[:, None] == jnp.arange(row_count, dtype=jnp.int32)[None, :]).astype(jnp.int32)
     row_rank = jnp.sum((jnp.cumsum(row_hot, axis=0) - row_hot) * row_hot, axis=1)

time: 329 us -> 322 us (0.979)
  waiting for transfers between devices: 241 us -> 235 us
    all_to_all x1, waiting for transfers between devices: 69.2 us -> 63.6 us  [packed(): arrived = lax.all_to_all(outgoing, 'x', 0, 0, tiled=True)]
where the time goes in v11:
time: 322 us
  waiting for transfers between devices  235 us (73%)
  matrix products  27.2 us (8%)
  local copies, waits for them, and re-layouts  18.8 us (6%)
  starting transfers between devices  15.4 us (5%)
  between operations  14.9 us (5%)
  other arithmetic  10.1 us (3%)
    all_gather x1, waiting for transfers between devices, on_device(): every_slot = lax.all_gather(weights_low, ('x', 'z'), axis=0, tiled=True)  95 us
    all_to_all x1, waiting for transfers between devices, packed(): arrived = lax.all_to_all(outgoing, 'x', 0, 0, tiled=True)  63.6 us
    reduce_scatter x1, waiting for transfers between devices, on_device(): gradient = lax.psum_scatter(row_sum, 'z', scatter_dimension=0, tiled=True)  59.5 us
    dot_general x13, matrix products, matmul(): jnp.einsum('srt,stu->sru', left, right, precision=lax.Precision.HIGHEST,...  18.7 us
    ppermute x3, waiting for transfers between devices, own_sum(): lax.ppermute(jnp.take(quarters, chip ^ shift, axis=1, mode='clip'), 'own'...  8.42 us
    gather x1, local copies, waits for them, and re-layouts, packed(): outgoing = jnp.take(rows, send_index, axis=0, mode='clip')  8.06 us
    gather x1, local copies, waits for them, and re-layouts, on_device(): weights = jnp.take(every_slot, target, axis=0, mode='clip')  6.48 us
  transfers between devices with their start and end apart: 11, of which 10 were waited for; matrix products, arithmetic and copies ran while one was open for 0% of the time, Pallas kernels for 0%

profile of v11, /device:TPU:1, one launch (start us, length us, event | category | flops | bytes accessed | tf_op | source)
XLA Modules:
  0.0 322.0 jit_solution(13552378378719430451)
XLA Ops:
  12.1 84.4 %conditional.1 = (f32[32,256,128]{2,1,0:T(8,128)}) conditional(s32[]{:T(128)} %convert_element_type.30, (pred[32]{0:T(512)(128)(4,1)S(1)}, pred[128,64]{1,0:T(8,128)(4,1)S(1)}, s32[128,64]{1,0:T(8,128)S(1)}, bf16[64,256,128]{2,1,0:T(8,128)(2,1)}) %tuple.81, (s32[64]{0:T(128)S(1)}, s32[64]{0:T(128)S(1)}, s32[]{:T(128)}, s32[64,4]{1,0:T(8,128)S(1)}, ...), branch_computations={%region_6.9_spmd, %region_9.14_spmd} | conditional | flops 8405888 | bytes 54572584 | solution.py:151
  12.3 8.1 %gather_fusion.1 = bf16[88,256,128]{2,1,0:T(8,128)(2,1)} fusion(bf16[64,256,128]{2,1,0:T(8,128)(2,1)} %get-tuple-element.91, s32[1024]{0:T(1024)S(1)} %pad_clamp_fusion.2), kind=kCustom, calls=%fused_computation.1 | custom fusion | bytes 11534688 | tf_op jit(solution)/shard_map/cond/branch_1_fun/jit(_take)/gather | solution.py:140
  20.4 5.1 %all-to-all-start.1 = ((bf16[4,22,256,128]{3,2,1,0:T(8,128)(2,1)}), bf16[4,22,256,128]{3,2,1,0:T(8,128)(2,1)}, u32[]{:S(2)}, u32[]{:S(2)}) async-start(bf16[4,22,256,128]{3,2,1,0:T(8,128)(2,1)} %bitcast.87), calls=%async_computation.1 | async-start | bytes 11534336 | tf_op jit(solution)/shard_map/cond/branch_1_fun/all_to_all | solution.py:142
  25.7 63.6 %all-to-all-done.1 = bf16[4,22,256,128]{3,2,1,0:T(8,128)(2,1)} async-done(((bf16[4,22,256,128]{3,2,1,0:T(8,128)(2,1)}), bf16[4,22,256,128]{3,2,1,0:T(8,128)(2,1)}, u32[]{:S(2)}, u32[]{:S(2)}) %all-to-all-start.1) | async-done | bytes 5767200 | tf_op jit(solution)/shard_map/cond/branch_1_fun/all_to_all | solution.py:142
  89.3 4.0 %convert_reduce_fusion.1 = f32[22,256,128]{2,1,0:T(8,128)S(1)} fusion(bf16[4,22,256,128]{3,2,1,0:T(8,128)(2,1)} %all-to-all-done.1), kind=kLoop, calls=%fused_computation.10 | loop fusion | flops 5046272 | bytes 8650752 | tf_op jit(solution)/shard_map/cond/branch_1_fun/reduce_sum | solution.py:143
  93.6 2.8 gather_fusion.2
  96.5 59.5 %reduce-scatter.2.cloned.1.call-done = f32[4,256,128]{2,1,0:T(8,128)} async-done(((f32[32,256,128]{2,1,0:T(8,128)}), f32[4,256,128]{2,1,0:T(8,128)}) %reduce-scatter.2.cloned.1.call-update) | async-done | bytes 524304 | tf_op jit(solution)/shard_map/reduce_scatter | solution.py:152
  156.0 2.3 fusion.14
  159.2 1.5 collective-permute-done
  162.2 2.5 collective-permute-start.2
  165.7 5.1 %collective-permute-done.2 = f32[4,32,256]{2,1,0:T(8,128)S(1)} collective-permute-done((f32[4,32,256]{2,1,0:T(8,128)S(1)}, f32[4,32,256]{2,1,0:T(8,128)S(1)}, u32[]{:S(2)}, u32[]{:S(2)}) %collective-permute-start.2) | collective-permute-done | bytes 131104 | tf_op jit(solution)/shard_map/ppermute | solution.py:66
  170.8 2.5 collective-permute-done.3
  173.6 1.5 collective-permute-start.5
  175.2 2.3 collective-permute-start.6
  177.5 3.2 %collective-permute-done.5 = f32[4,32,256]{2,1,0:T(8,128)S(1)} collective-permute-done((f32[4,32,256]{2,1,0:T(8,128)S(1)}, f32[4,32,256]{2,1,0:T(8,128)S(1)}, u32[]{:S(2)}, u32[]{:S(2)}) %collective-permute-start.5) | collective-permute-done | bytes 131104 | tf_op jit(solution)/shard_map/ppermute | solution.py:72
  180.7 2.6 collective-permute-done.6
  188.3 22.1 %while.18 = (s32[]{:T(128)}, f32[4,256,128]{2,1,0:T(8,128)S(1)}, f32[4,256,256]{2,1,0:T(8,128)S(1)}, s32[]{:T(128)}) while((s32[]{:T(128)}, f32[4,256,128]{2,1,0:T(8,128)S(1)}, f32[4,256,256]{2,1,0:T(8,128)S(1)}, s32[]{:T(128)}) %tuple.72), condition=%wide.region_17.18_spmd.clone, body=%wide.region_16.17_spmd.clone.sunk | while | flops 2820276224 | bytes 12320821 | solution.py:161
  189.5 1.9 fusion.55
  195.1 1.9 fusion.55
  200.6 1.9 fusion.55
  206.2 1.9 fusion.55
  211.7 2.0 fusion.24
  213.7 95.0 %all-gather.2.cloned.1.call-done = bf16[128,256,128]{2,1,0:T(8,128)(2,1)} async-done(((bf16[4,256,128]{2,1,0:T(8,128)(2,1)}), bf16[128,256,128]{2,1,0:T(8,128)(2,1)}) %all-gather.2.cloned.1.call-update) | async-done | bytes 8388624 | tf_op jit(solution)/shard_map/all_gather | solution.py:168
  308.7 6.5 %gather_fusion.4 = bf16[64,256,128]{2,1,0:T(8,128)(2,1)} fusion(bf16[128,256,128]{2,1,0:T(8,128)(2,1)} %all-gather.2.cloned.1.call-done, s32[1024]{0:T(1024)S(1)} %pad_clamp_fusion.3), kind=kCustom, calls=%fused_computation.4 | custom fusion | bytes 8388864 | tf_op jit(solution)/shard_map/jit(_take)/gather | solution.py:169
  (78 shorter events, 29.1 us)
Async XLA Ops:
  7.2 148.9 %reduce-scatter.2.cloned.1.call-start = ((), (), s32[]{:S(2)}) async-start(), calls=%async_computation.3 | async-start | bytes 4718592 | tf_op jit(solution)/shard_map/reduce_scatter | solution.py:152
  20.4 68.9 %all-to-all-start.1 = ((bf16[4,22,256,128]{3,2,1,0:T(8,128)(2,1)}), bf16[4,22,256,128]{3,2,1,0:T(8,128)(2,1)}, u32[]{:S(2)}, u32[]{:S(2)}) async-start(bf16[4,22,256,128]{3,2,1,0:T(8,128)(2,1)} %bitcast.87), calls=%async_computation.1 | async-start | bytes 11534336 | tf_op jit(solution)/shard_map/cond/branch_1_fun/all_to_all | solution.py:142
  96.5 59.6 %copy-start = (f32[1,4,256,128]{3,2,1,0:T(8,128)S(1)}, f32[1,4,256,128]{3,2,1,0:T(8,128)}, u32[]{:S(2)}) copy-start(f32[1,4,256,128]{3,2,1,0:T(8,128)} %param.10) | copy-start | bytes 1572868
  96.5 212.2 %all-gather.2.cloned.1.call-start = ((), (), s32[]{:S(2)}) async-start(), calls=%async_computation.4 | async-start | bytes 8650752 | tf_op jit(solution)/shard_map/all_gather | solution.py:168
  158.4 2.4 collective-permute-start
  160.9 26.4 %copy-start.1 = (f32[4,256,128]{2,1,0:T(8,128)S(1)}, f32[4,256,128]{2,1,0:T(8,128)}, u32[]{:S(2)}) copy-start(f32[4,256,128]{2,1,0:T(8,128)} %reduce-scatter.2.cloned.1.call-done) | copy-start | bytes 1572868
  160.9 4.8 %collective-permute-start.1 = (f32[4,32,256]{2,1,0:T(8,128)S(1)}, f32[4,32,256]{2,1,0:T(8,128)S(1)}, u32[]{:S(2)}, u32[]{:S(2)}) collective-permute-start(f32[4,32,256]{2,1,0:T(8,128)S(1)} %get-tuple-element.238), channel_id=1, source_target_pairs={{0,2},{1,3},{2,0},{3,1},{4,6},{5,7},{6,4},{7,5},{8,10},{9,11},{10,... | collective-permute-start | bytes 393224 | tf_op jit(solution)/shard_map/ppermute | solution.py:66
  162.2 8.5 %collective-permute-start.2 = (f32[4,32,256]{2,1,0:T(8,128)S(1)}, f32[4,32,256]{2,1,0:T(8,128)S(1)}, u32[]{:S(2)}, u32[]{:S(2)}) collective-permute-start(f32[4,32,256]{2,1,0:T(8,128)S(1)} %get-tuple-element.240), channel_id=1, source_target_pairs={{0,4},{1,5},{2,6},{3,7},{4,0},{5,1},{6,2},{7,3},{8,12},{9,13},{10,... | collective-permute-start | bytes 393224 | tf_op jit(solution)/shard_map/ppermute | solution.py:66
  164.7 8.6 %collective-permute-start.3 = (f32[4,32,256]{2,1,0:T(8,128)S(1)}, f32[4,32,256]{2,1,0:T(8,128)S(1)}, u32[]{:S(2)}, u32[]{:S(2)}) collective-permute-start(f32[4,32,256]{2,1,0:T(8,128)S(1)} %get-tuple-element.239), channel_id=1, source_target_pairs={{0,6},{1,7},{2,4},{3,5},{4,2},{5,3},{6,0},{7,1},{8,14},{9,15},{10,... | collective-permute-start | bytes 393224 | tf_op jit(solution)/shard_map/ppermute | solution.py:66
  173.3 4.1 %collective-permute-start.4 = (f32[4,32,256]{2,1,0:T(8,128)S(1)}, f32[4,32,256]{2,1,0:T(8,128)S(1)}, u32[]{:S(2)}, u32[]{:S(2)}) collective-permute-start(f32[4,32,256]{2,1,0:T(8,128)S(1)} %fusion.16), channel_id=1, source_target_pairs={{0,2},{1,3},{2,0},{3,1},{4,6},{5,7},{6,4},{7,5},{8,10},{9,11},{10,... | collective-permute-start | bytes 393224 | tf_op jit(solution)/shard_map/ppermute | solution.py:72
  173.6 7.1 %collective-permute-start.5 = (f32[4,32,256]{2,1,0:T(8,128)S(1)}, f32[4,32,256]{2,1,0:T(8,128)S(1)}, u32[]{:S(2)}, u32[]{:S(2)}) collective-permute-start(f32[4,32,256]{2,1,0:T(8,128)S(1)} %fusion.16), channel_id=1, source_target_pairs={{0,4},{1,5},{2,6},{3,7},{4,0},{5,1},{6,2},{7,3},{8,12},{9,13},{10,... | collective-permute-start | bytes 393224 | tf_op jit(solution)/shard_map/ppermute | solution.py:72
  175.2 8.2 %collective-permute-start.6 = (f32[4,32,256]{2,1,0:T(8,128)S(1)}, f32[4,32,256]{2,1,0:T(8,128)S(1)}, u32[]{:S(2)}, u32[]{:S(2)}) collective-permute-start(f32[4,32,256]{2,1,0:T(8,128)S(1)} %fusion.16), channel_id=1, source_target_pairs={{0,6},{1,7},{2,4},{3,5},{4,2},{5,3},{6,0},{7,1},{8,14},{9,15},{10,... | collective-permute-start | bytes 393224 | tf_op jit(solution)/shard_map/ppermute | solution.py:72
  184.0 2.8 collective-permute-start.7
  188.3 23.4 %copy-start.2 = (f32[1,4,256,128]{3,2,1,0:T(8,128)S(1)}, f32[1,4,256,128]{3,2,1,0:T(8,128)}, u32[]{:S(2)}) copy-start(f32[1,4,256,128]{3,2,1,0:T(8,128)} %param.11) | copy-start | bytes 1572868
Sparse Core Ops, SparseCore 0:
  96.6 59.3 reduce-scatter.1
  213.8 94.8 all-gather.1
